TPU v7x, 256 devices: a whole 4x4x8 slice. The times are simulated.
256 devices in a mesh: replica: 16 (over z_lo, x, core), shard: 16 (over z_hi, y).
Axes of the slice: x: 4, y: 4, z: 8 (z_hi: 4, z_lo: 2; z = z_hi * 2 + z_lo), core: 2. Of those that a mesh axis runs over, the one named last changes fastest.
Arguments:
- tokens: bfloat16 [32768, 8192], P(('replica', 'shard')), may hold values from -6 to 6
- query_vectors: bfloat16 [32768, 8192], P(('replica', 'shard')), may hold values from -4.5 to 4.5
- key_vectors: bfloat16 [32768, 1024], P(('replica', 'shard')), may hold values from -4.5 to 4.5
- segment_ids: int32 [256, 128], P(('replica', 'shard')), may hold values from 0 to 7, never falling along the last dimension, each value on 1 to 32 neighbouring positions
- base_weight: bfloat16 [8192, 1024], P('shard'), may hold values from -0.0625 to 0.0625
- delta_values: bfloat16 [64, 64, 64], replicated, may hold values from -0.1875 to 0.1875
- block_list: int32 [64, 2], replicated, may hold values from 0 to 127, as said below
- out_cotangent: bfloat16 [32768, 8192], P(('replica', 'shard')), may hold values from -6 to 6
Outputs:
- attention: bfloat16 [32768, 8192], P(('replica', 'shard'))
- input_grad: bfloat16 [32768, 8192], P(('replica', 'shard'))
- delta_grad: float32 [64, 64, 64], P('shard')
Inputs may be any that keep to these rules, and one draw needn't show every extreme that they name: `segment_ids`: segment ids never fall along a row; each row is the tokens of one device. `block_list`: every row names a distinct pair (row block below 128, column block below 16).
All inputs are finite; a program needn't handle non-finite values.
Results may differ from a plain program's by a relative error of at most 0.0056.
Values may be sent and summed in bfloat16 or wider, within the bound.
No kernel may reach another device: no remote copies, remote signals or barrier semaphores. Data moves between devices by JAX's collectives and lax.ppermute only.
A program may use at most 128 MiB of HBM per device.

v0:
```python
import math

import jax
import jax.numpy as jnp
from jax import lax
from jax.sharding import PartitionSpec as P

D = 8192
QH = 64
KVH = 8
HD = 128
BLK = 64


def block_tables(block_list):
    row_hot = (block_list[:, 0:1] == jnp.arange(D // BLK, dtype=jnp.int32)[None, :]).astype(
        jnp.bfloat16
    )
    col_hot = (block_list[:, 1:2] == jnp.arange(KVH * HD // BLK, dtype=jnp.int32)[None, :]).astype(
        jnp.bfloat16
    )
    return (row_hot, col_hot)


def local(
    tokens,
    query_vectors,
    key_vectors,
    segment_ids,
    base_weight,
    delta_values,
    block_list,
    out_cotangent,
):
    tok_rows = tokens.shape[0]
    groups = QH // KVH
    row_index = block_list[:, 0]
    col_index = block_list[:, 1]
    row_hot, col_hot = block_tables(block_list)
    picked = jnp.einsum(
        "trk,br->tbk",
        tokens.reshape(tok_rows, D // BLK, BLK),
        row_hot,
        preferred_element_type=jnp.float32,
    ).astype(jnp.bfloat16)
    block_term = jnp.einsum(
        "tbk,bkj->tbj", picked, delta_values, preferred_element_type=jnp.float32
    )
    sparse_part = (
        jnp.zeros((tok_rows, KVH * HD // BLK, BLK), jnp.float32)
        .at[:, col_index]
        .add(block_term)
        .reshape(tok_rows, KVH * HD)
    )
    full_weight = lax.all_gather(base_weight, "shard", axis=0, tiled=True)
    dense_part = jnp.dot(tokens, full_weight, preferred_element_type=jnp.float32)
    values = (dense_part + sparse_part).astype(jnp.bfloat16)
    query_heads = query_vectors.reshape(tok_rows, KVH, groups, HD)
    key_heads = key_vectors.reshape(tok_rows, KVH, HD)
    scores = jnp.einsum(
        "tgsd,ugd->gstu", query_heads, key_heads, preferred_element_type=jnp.float32
    ) * (1.0 / math.sqrt(HD))
    seg_row = segment_ids[0]
    position = jnp.arange(tok_rows, dtype=jnp.int32)
    allowed = (position[None, :] <= position[:, None]) & (seg_row[:, None] == seg_row[None, :])
    scores = jnp.where(allowed, scores, -1e30)
    row_max = jnp.max(scores, axis=-1, keepdims=True)
    exp_scores = jnp.exp(scores - row_max)
    attn_probs = (exp_scores / jnp.sum(exp_scores, axis=-1, keepdims=True)).astype(jnp.bfloat16)
    value_heads = values.reshape(tok_rows, KVH, HD)
    attention = (
        jnp.einsum("gstu,ugd->tgsd", attn_probs, value_heads, preferred_element_type=jnp.float32)
        .reshape(tok_rows, QH * HD)
        .astype(jnp.bfloat16)
    )
    cotangent_heads = out_cotangent.reshape(tok_rows, KVH, groups, HD)
    value_grad = (
        jnp.einsum(
            "gstu,tgsd->ugd", attn_probs, cotangent_heads, preferred_element_type=jnp.float32
        )
        .reshape(tok_rows, KVH * HD)
        .astype(jnp.bfloat16)
    )
    dense_back = lax.dot_general(
        value_grad, full_weight, (((1,), (1,)), ((), ())), preferred_element_type=jnp.float32
    )
    chosen = jnp.einsum(
        "tcj,bc->tbj",
        value_grad.reshape(tok_rows, KVH * HD // BLK, BLK),
        col_hot,
        preferred_element_type=jnp.float32,
    ).astype(jnp.bfloat16)
    back_term = jnp.einsum("tbj,bkj->tbk", chosen, delta_values, preferred_element_type=jnp.float32)
    spread_back = (
        jnp.zeros((tok_rows, D // BLK, BLK), jnp.float32)
        .at[:, row_index]
        .add(back_term)
        .reshape(tok_rows, D)
    )
    input_grad = (dense_back + spread_back).astype(jnp.bfloat16)
    grad_scale = 1.0 / math.sqrt(tok_rows * lax.axis_size("replica") * lax.axis_size("shard"))
    grad_term = (
        jnp.einsum("tbk,tbj->bkj", picked, chosen, preferred_element_type=jnp.float32) * grad_scale
    )
    grad_whole = lax.psum(grad_term, "replica")
    delta_grad = lax.psum_scatter(grad_whole, "shard", scatter_dimension=0, tiled=True)
    return (attention, input_grad, delta_grad)


def solution(mesh):
    return jax.shard_map(
        local,
        mesh=mesh,
        in_specs=(
            P(("replica", "shard"), None),
            P(("replica", "shard"), None),
            P(("replica", "shard"), None),
            P(("replica", "shard"), None),
            P("shard", None),
            P(),
            P(),
            P(("replica", "shard"), None),
        ),
        out_specs=(
            P(("replica", "shard"), None),
            P(("replica", "shard"), None),
            P("shard", None, None),
        ),
        check_vma=False,
    )
```

profile of v0, /device:TPU:1, one launch (start us, length us, event | category | flops | bytes accessed | tf_op | source)
XLA Modules:
  0.0 457.5 jit_solution(6731068299304042135)
XLA Ops:
  7.2 0.0 copy-start
  7.2 0.0 reduce-scatter.2.cloned.1.call-start
  7.2 0.0 copy-start.7
  7.2 0.0 copy-start.8
  7.2 3.6 copy.55
  10.9 0.0 copy-done.7
  10.9 0.0 copy-done.8
  10.9 0.1 fusion.27
  11.0 0.0 copy-start.9
  11.0 0.0 copy-start.2
  11.0 4.2 copy.53
  15.3 0.0 copy-done.9
  15.3 0.0 copy-done.2
  15.3 2.4 copy.27
  17.7 3.2 fusion.3
  21.0 1.1 fusion.38
  22.0 0.0 copy-start.5
  22.1 0.6 divide_convert_fusion
  22.7 1.0 copy-done.5
  23.6 0.7 fusion.17
  24.4 0.5 fusion.13
  24.8 0.0 copy-start.4
  24.9 0.4 copy-done.6
  25.2 1.5 fusion.14
  26.7 1.0 copy-done.3
  27.8 2.7 convolution_multiply_fusion
  30.5 0.0 reduce-scatter.2.cloned.1.call-update
  30.6 0.0 all-gather.2.cloned.1.call-start
  30.6 0.7 all-gather.2.cloned.1.call-update
  31.3 0.2 all-reduce.2.cloned.1.call-start
  31.5 0.0 copy-done
  31.5 3.6 fusion.20
  35.1 2.5 broadcast_in_dim.25
  37.6 10.4 %scatter_fusion.1 = f32[128,128,64]{0,2,1:T(8,128)} fusion(f32[128,128,64]{0,2,1:T(8,128)} %broadcast_in_dim.25, s32[64]{0:T(128)S(1)} %get-tuple-element.11, f32[64,128,64]{1,2,0:T(8,128)} %fusion.20), kind=kCustom, calls=%fused_computation.1 | custom fusion | flops 524288 | bytes 6291712 | tf_op jit(solution)/shard_map/scatter-add | solution.py:97
  48.1 5.6 %copy.40 = f32[128,8192]{1,0:T(8,128)} copy(f32[128,8192]{0,1:T(8,128)} %bitcast.70) | data formatting | bytes 8388608 | tf_op jit(solution)/shard_map/reshape | solution.py:98
  53.7 3.8 fusion.23
  57.5 7.0 %scatter_fusion = f32[128,16,64]{0,2,1:T(8,128)S(1)} fusion(f32[128,16,64]{0,2,1:T(8,128)S(1)} %broadcast_in_dim.12, s32[64]{0:T(128)S(1)} %get-tuple-element.10, f32[64,128,64]{1,2,0:T(8,128)} %fusion.23), kind=kCustom, calls=%fused_computation | custom fusion | flops 524288 | bytes 6291712 | tf_op jit(solution)/shard_map/scatter-add | solution.py:52
  64.6 0.2 copy.31
  64.8 57.4 %reduce-scatter.2.cloned.1.call-done = f32[4,64,64]{2,1,0:T(8,128)} async-done(((f32[64,64,64]{2,1,0:T(8,128)}), f32[4,64,64]{2,1,0:T(8,128)}) %reduce-scatter.2.cloned.1.call-update) | async-done | bytes 65552 | tf_op jit(solution)/shard_map/reduce_scatter | solution.py:106
  122.2 0.0 all-reduce.2.cloned.1.call-update
  122.2 202.9 %all-gather.2.cloned.1.call-done = bf16[8192,1024]{1,0:T(8,128)(2,1)} async-done(((bf16[512,1024]{1,0:T(8,128)(2,1)}), bf16[8192,1024]{1,0:T(8,128)(2,1)}) %all-gather.2.cloned.1.call-update) | async-done | bytes 16777232 | tf_op jit(solution)/shard_map/all_gather | solution.py:55
  325.1 8.7 %fusion.18 = bf16[128,1024]{1,0:T(8,128)(2,1)S(1)} fusion(f32[128,1024]{1,0:T(8,128)S(1)} %copy.31, bf16[128,8192]{1,0:T(8,128)(2,1)} %param.8, bf16[8192,1024]{1,0:T(8,128)(2,1)} %all-gather.2.cloned.1.call-done), kind=kOutput, calls=%fused_computation.25 | convolution fusion | flops 2147745792 | bytes 19660800 | tf_op jit(solution)/shard_map/dot_general | solution.py:56
  333.9 0.2 copy.50
  334.1 14.0 %fusion.1 = bf16[128,8192]{1,0:T(8,128)(2,1)} fusion(f32[128,8192]{1,0:T(8,128)} %copy.40, bf16[128,1024]{0,1:T(8,128)(2,1)S(1)} %bitcast.76, bf16[8192,1024]{1,0:T(8,128)(2,1)} %all-gather.2.cloned.1.call-done), kind=kOutput, calls=%fused_computation.4 | convolution fusion | flops 2149580800 | bytes 23330816 | tf_op jit(solution)/shard_map/dot_general | solution.py:84
  348.0 2.0 convolution_convert_fusion
  350.1 4.2 copy.43
  354.2 95.1 %all-reduce.2.cloned.1.call-done = f32[4,64,64]{2,1,0:T(8,128)} async-done(((f32[4,64,64]{2,1,0:T(8,128)}), f32[4,64,64]{2,1,0:T(8,128)}) %all-reduce.2.cloned.1.call-update) | async-done | bytes 65552 | tf_op jit(solution)/shard_map/psum | solution.py:105
  449.4 1.6 copy.79
  (8 shorter events, 0.1 us)
Async XLA Ops:
  7.2 24.4 %copy-start = (bf16[64,64,64]{2,1,0:T(8,128)(2,1)S(1)}, bf16[64,64,64]{2,1,0:T(8,128)(2,1)}, u32[]{:S(2)}) copy-start(bf16[64,64,64]{2,1,0:T(8,128)(2,1)} %param.13) | copy-start | bytes 1572868
  7.2 115.0 %reduce-scatter.2.cloned.1.call-start = ((), (), s32[]{:S(2)}) async-start(), calls=%async_computation.2 | async-start | bytes 2228224 | tf_op jit(solution)/shard_map/reduce_scatter | solution.py:106
  7.2 3.6 copy-start.7
  7.2 3.7 copy-start.8
  11.0 4.2 copy-start.9
  11.0 4.2 copy-start.2
  22.0 1.6 copy-start.5
  23.6 1.6 copy-start.6
  24.8 1.9 copy-start.4
  26.7 1.0 copy-start.3
  30.6 294.6 %all-gather.2.cloned.1.call-start = ((), (), s32[]{:S(2)}) async-start(), calls=%async_computation.1 | async-start | bytes 17825792 | tf_op jit(solution)/shard_map/all_gather | solution.py:55
  31.3 418.1 %all-reduce.2.cloned.1.call-start = ((), (), s32[]{:S(2)}) async-start(), calls=%async_computation.3 | async-start | bytes 262144 | tf_op jit(solution)/shard_map/psum | solution.py:105
  350.1 100.9 %copy-start.1 = (bf16[64,64,64]{2,1,0:T(8,128)(2,1)S(1)}, bf16[64,64,64]{2,1,0:T(8,128)(2,1)}, u32[]{:S(2)}) copy-start(bf16[64,64,64]{2,1,0:T(8,128)(2,1)} %param.13) | copy-start | bytes 1572868
Sparse Core Ops, SparseCore 0:
  30.7 91.5 reduce-scatter.1
  124.7 200.4 all-gather.1
  327.8 121.5 all-reduce.1
where the time goes:
time: 458 us; the launch traced here: 457 us
  waiting for transfers between devices  356 us (78%)
  matrix products  40.8 us (9%)
  local copies, waits for them, and re-layouts  27 us (6%)
  other arithmetic  19.3 us (4%)
  between operations  13.9 us (3%)
    all_gather x1, waiting for transfers between devices, local(): full_weight = lax.all_gather(base_weight, 'shard', axis=0, tiled=True)  203 us
    psum x1, waiting for transfers between devices, local(): grad_whole = lax.psum(grad_term, 'replica')  95.1 us
    reduce_scatter x1, waiting for transfers between devices, local(): lax.psum_scatter(grad_whole, 'shard', scatter_dimension=0, tiled=True)  57.4 us
    unnamed x25, local copies, waits for them, and re-layouts  14.2 us
    dot_general x1, matrix products, local(): lax.dot_general(value_grad, full_weight, (((1,), (1,)), ((), ())), prefer...  14 us
    scatter-add x1, other arithmetic, local(): spread_back = jnp.zeros((tok_rows, D // BLK, BLK), jnp.float32).at[:, row...  10.4 us
  transfers between devices with their start and end apart: 3, of which 3 were waited for; matrix products, arithmetic and copies ran while one was open for 14% of the time, Pallas kernels for 0%

commit v1 on v0

v1 whole, which is shorter than its diff:
```python
import math

import jax
import jax.numpy as jnp
from jax import lax
from jax.sharding import Mesh
from jax.sharding import PartitionSpec as P

D = 8192
QH = 64
KVH = 8
HD = 128
BLK = 64

REPLICA = ("zl", "x", "c")
SHARD = ("zh", "y")
ALL = REPLICA + SHARD
PIECE = ("x", "c")


def block_tables(block_list):
    row_hot = (block_list[:, 0:1] == jnp.arange(D // BLK, dtype=jnp.int32)[None, :]).astype(
        jnp.bfloat16
    )
    col_hot = (block_list[:, 1:2] == jnp.arange(KVH * HD // BLK, dtype=jnp.int32)[None, :]).astype(
        jnp.bfloat16
    )
    return (row_hot, col_hot)


def gather_weight(base_weight):
    rows = base_weight.shape[0]
    pieces = lax.axis_size("x") * lax.axis_size("c")
    width = rows // pieces
    me = lax.axis_index("x") * lax.axis_size("c") + lax.axis_index("c")
    piece = lax.dynamic_slice_in_dim(base_weight, me * width, width, 0)
    by_shard = lax.all_gather(piece, SHARD, axis=0, tiled=False)
    whole = lax.all_gather(by_shard, PIECE, axis=1, tiled=True)
    return whole.reshape(-1, base_weight.shape[1])


def reduce_delta(grad_term):
    n_shard = lax.axis_size(SHARD)
    n_rep = lax.axis_size(REPLICA)
    nb = grad_term.shape[0]
    flat = grad_term.reshape(n_shard, -1)
    mine = lax.all_to_all(flat, SHARD, 0, 0, tiled=False).sum(0)
    mine = mine.reshape(n_rep, -1)
    part = lax.all_to_all(mine, REPLICA, 0, 0, tiled=False).sum(0)
    spread = jnp.broadcast_to(part[None], (n_rep,) + part.shape)
    whole = lax.all_to_all(spread, REPLICA, 0, 0, tiled=False)
    return whole.reshape(nb // n_shard, BLK, BLK)


def local(
    tokens,
    query_vectors,
    key_vectors,
    segment_ids,
    base_weight,
    delta_values,
    block_list,
    out_cotangent,
):
    tok_rows = tokens.shape[0]
    groups = QH // KVH
    row_index = block_list[:, 0]
    col_index = block_list[:, 1]
    full_weight = gather_weight(base_weight)
    row_hot, col_hot = block_tables(block_list)
    picked = jnp.einsum(
        "trk,br->tbk",
        tokens.reshape(tok_rows, D // BLK, BLK),
        row_hot,
        preferred_element_type=jnp.float32,
    ).astype(jnp.bfloat16)
    query_heads = query_vectors.reshape(tok_rows, KVH, groups, HD)
    key_heads = key_vectors.reshape(tok_rows, KVH, HD)
    scores = jnp.einsum(
        "tgsd,ugd->gstu", query_heads, key_heads, preferred_element_type=jnp.float32
    ) * (1.0 / math.sqrt(HD))
    seg_row = segment_ids[0]
    position = jnp.arange(tok_rows, dtype=jnp.int32)
    allowed = (position[None, :] <= position[:, None]) & (seg_row[:, None] == seg_row[None, :])
    scores = jnp.where(allowed, scores, -1e30)
    row_max = jnp.max(scores, axis=-1, keepdims=True)
    exp_scores = jnp.exp(scores - row_max)
    attn_probs = (exp_scores / jnp.sum(exp_scores, axis=-1, keepdims=True)).astype(jnp.bfloat16)
    cotangent_heads = out_cotangent.reshape(tok_rows, KVH, groups, HD)
    value_grad = (
        jnp.einsum(
            "gstu,tgsd->ugd", attn_probs, cotangent_heads, preferred_element_type=jnp.float32
        )
        .reshape(tok_rows, KVH * HD)
        .astype(jnp.bfloat16)
    )
    chosen = jnp.einsum(
        "tcj,bc->tbj",
        value_grad.reshape(tok_rows, KVH * HD // BLK, BLK),
        col_hot,
        preferred_element_type=jnp.float32,
    ).astype(jnp.bfloat16)
    grad_scale = 1.0 / math.sqrt(tok_rows * lax.axis_size(ALL))
    grad_term = (
        jnp.einsum("tbk,tbj->bkj", picked, chosen, preferred_element_type=jnp.float32) * grad_scale
    )
    delta_grad = reduce_delta(grad_term)

    block_term = jnp.einsum(
        "tbk,bkj->tbj", picked, delta_values, preferred_element_type=jnp.float32
    )
    sparse_part = (
        jnp.zeros((tok_rows, KVH * HD // BLK, BLK), jnp.float32)
        .at[:, col_index]
        .add(block_term)
        .reshape(tok_rows, KVH * HD)
    )
    dense_part = jnp.dot(tokens, full_weight, preferred_element_type=jnp.float32)
    values = (dense_part + sparse_part).astype(jnp.bfloat16)
    value_heads = values.reshape(tok_rows, KVH, HD)
    attention = (
        jnp.einsum("gstu,ugd->tgsd", attn_probs, value_heads, preferred_element_type=jnp.float32)
        .reshape(tok_rows, QH * HD)
        .astype(jnp.bfloat16)
    )
    dense_back = lax.dot_general(
        value_grad, full_weight, (((1,), (1,)), ((), ())), preferred_element_type=jnp.float32
    )
    back_term = jnp.einsum("tbj,bkj->tbk", chosen, delta_values, preferred_element_type=jnp.float32)
    spread_back = (
        jnp.zeros((tok_rows, D // BLK, BLK), jnp.float32)
        .at[:, row_index]
        .add(back_term)
        .reshape(tok_rows, D)
    )
    input_grad = (dense_back + spread_back).astype(jnp.bfloat16)
    return (attention, input_grad, delta_grad)


def solution(mesh):
    n_shard = mesh.shape["shard"]
    n_rep = mesh.shape["replica"]
    fine = Mesh(
        mesh.devices.reshape(2, 4, n_rep // 8, 4, n_shard // 4), ALL
    )
    tok = P(ALL, None)
    return jax.shard_map(
        local,
        mesh=fine,
        in_specs=(tok, tok, tok, tok, P(SHARD, None), P(), P(), tok),
        out_specs=(tok, tok, P(SHARD, None, None)),
        check_vma=False,
    )
```

time: 458 us -> 221 us (0.48)
  waiting for transfers between devices: 356 us -> 66.1 us
  blocking collectives: 0 us -> 33.1 us
  starting transfers between devices: 0.3 us -> 10.8 us
  local copies, waits for them, and re-layouts: 27 us -> 32.1 us
    all_gather x1 -> x2, waiting for transfers between devices: 203 us -> 63.8 us  [the longest x1 63.8 us: gather_weight(): by_shard = lax.all_gather(piece, SHARD, axis=0, tiled=False)]
    psum x1 -> x0, waiting for transfers between devices: 95.1 us -> none  [local(): grad_whole = lax.psum(grad_term, 'replica')]
    reduce_scatter x1 -> x0, waiting for transfers between devices: 57.4 us -> none  [local(): lax.psum_scatter(grad_whole, 'shard', scatter_dimension=0, tiled=True)]
    all_to_all x0 -> x1, blocking collectives: none -> 33.1 us  [reduce_delta(): mine = lax.all_to_all(flat, SHARD, 0, 0, tiled=False).sum(0)]
    all_to_all x0 -> x2, starting transfers between devices: none -> 10.8 us  [the longest x1 7.02 us: reduce_delta(): part = lax.all_to_all(mine, REPLICA, 0, 0, tiled=False).sum(0)]
    unnamed x25 -> x22, local copies, waits for them, and re-layouts: 14.2 us -> 13.4 us
  transfers between devices with their start and end apart: 3 -> 4, of which waited for: 3 -> 2; matrix products, arithmetic and copies ran while one was open for 14% -> 26% of each run, Pallas kernels for 0% -> 0%
where the time goes in v1:
time: 221 us; the launch traced here: 220 us
  waiting for transfers between devices  66.1 us (30%)
  matrix products  41.4 us (19%)
  blocking collectives  33.1 us (15%)
  local copies, waits for them, and re-layouts  32.1 us (15%)
  other arithmetic  22.1 us (10%)
  between operations  14.2 us (6%)
  starting transfers between devices  10.8 us (5%)
    all_gather x1, waiting for transfers between devices, gather_weight(): by_shard = lax.all_gather(piece, SHARD, axis=0, tiled=False)  63.8 us
    all_to_all x1, blocking collectives, reduce_delta(): mine = lax.all_to_all(flat, SHARD, 0, 0, tiled=False).sum(0)  33.1 us
    dot_general x1, matrix products, local(): lax.dot_general(value_grad, full_weight, (((1,), (1,)), ((), ())), prefer...  14 us
    unnamed x22, local copies, waits for them, and re-layouts  13.4 us
    dot_general x1, matrix products, local(): jnp.dot(tokens, full_weight, preferred_element_type=jnp.float32)  10.9 us
    scatter-add x1, other arithmetic, local(): spread_back = jnp.zeros((tok_rows, D // BLK, BLK), jnp.float32).at[:, row...  10.6 us
    scatter-add x1, other arithmetic, local(): sparse_part = jnp.zeros((tok_rows, KVH * HD // BLK, BLK), jnp.float32).at...  7.02 us
    all_to_all x1, starting transfers between devices, reduce_delta(): part = lax.all_to_all(mine, REPLICA, 0, 0, tiled=False).sum(0)  7.02 us
  transfers between devices with their start and end apart: 4, of which 2 were waited for; matrix products, arithmetic and copies ran while one was open for 26% of the time, Pallas kernels for 0%

profile of v1, /device:TPU:1, one launch (start us, length us, event | category | flops | bytes accessed | tf_op | source)
XLA Modules:
  0.0 219.9 jit_solution(9076998885968689169)
XLA Ops:
  7.2 0.0 copy-start
  7.2 0.0 copy-start.6
  7.2 0.0 all-gather.6.cloned.1.call-start
  7.2 1.7 constant_dynamic-slice_fusion
  8.9 0.0 all-gather.6.cloned.1.call-update
  8.9 0.0 all-gather.4.cloned.1.call-start
  9.0 63.8 %all-gather.6.cloned.1.call-done = bf16[1024,1024]{1,0:T(8,128)(2,1)} async-done(((bf16[64,1024]{1,0:T(8,128)(2,1)}), bf16[1024,1024]{1,0:T(8,128)(2,1)}) %all-gather.6.cloned.1.call-update) | async-done | bytes 2097168 | tf_op jit(solution)/shard_map/all_gather | solution.py:37
  72.8 0.0 all-gather.4.cloned.1.call-update
  72.8 0.0 copy-done.6
  72.9 2.2 copy.100
  75.1 4.1 %copy.97 = bf16[128,8192]{0,1:T(8,128)(2,1)} copy(bf16[128,8192]{1,0:T(8,128)(2,1)} %param.15) | data formatting | bytes 4194304 | tf_op jit(solution)/shard_map/reshape | solution.py:89
  79.2 4.1 %copy.72 = bf16[128,8192]{0,1:T(8,128)(2,1)} copy(bf16[128,8192]{1,0:T(8,128)(2,1)} %param.8) | data formatting | bytes 4194304 | tf_op args[0]
  83.3 0.0 copy-done.8
  83.3 0.0 copy-done.7
  83.3 0.1 fusion.28
  83.4 1.6 fusion.3
  85.0 1.1 fusion.39
  86.1 0.0 copy-start.5
  86.1 0.6 divide_convert_fusion
  86.7 1.3 copy-done.5
  88.0 0.7 fusion.18
  88.7 0.5 fusion.13
  89.2 0.7 copy-done.4
  89.9 1.5 fusion.14
  91.4 1.0 copy-done.2
  92.4 2.7 %convolution_multiply_fusion = f32[64,64,64]{2,1,0:T(8,128)} fusion(bf16[128,64,64]{0,1,2:T(8,128)(2,1)S(1)} %fusion.13, bf16[128,64,64]{0,1,2:T(8,128)(2,1)S(1)} %fusion.14), kind=kOutput, calls=%fused_computation.17 | convolution fusion | flops 67371008 | bytes 3145728 | tf_op jit(solution)/shard_map/tbk,tbj->bkj/dot_general | solution.py:105
  95.2 3.4 %all_to_all.21 = f32[16,1,16384]{2,1,0:T(1,128)} reshape(f32[64,64,64]{2,1,0:T(8,128)} %convolution_multiply_fusion) | data formatting | bytes 2097152 | tf_op jit(solution)/shard_map/all_to_all | solution.py:47
  98.6 33.1 %all_to_all.25 = f32[16,1,16384]{2,1,0:T(1,128)} all-to-all(f32[16,1,16384]{2,1,0:T(1,128)} %all_to_all.21), channel_id=1, replica_groups=mesh['zl'=2,'x'=4,'c'=2,'zh'=4,'y'=4] {'zh','y'}, dimensions={0} | all-to-all | bytes 2097152 | tf_op jit(solution)/shard_map/all_to_all | solution.py:47
  131.7 2.6 %reduce_sum.28 = f32[16384]{0:T(1024)} reduce(f32[16,1,16384]{2,1,0:T(1,128)} %all_to_all.25, f32[]{:T(128)} %constant.9.clone.1), dimensions={0,1}, to_apply=%region_4.5 | reduce | flops 245760 | bytes 1114116 | tf_op jit(solution)/shard_map/reduce_sum | solution.py:47
  134.2 7.0 %all-to-all-start.1 = ((f32[16,1,1024]{2,1,0:T(1,128)}), f32[16,1,1024]{2,1,0:T(1,128)S(1)}, u32[]{:S(2)}, u32[]{:S(2)}) async-start(f32[16,1,1024]{2,1,0:T(1,128)} %bitcast.28), calls=%async_computation.1 | async-start | bytes 131072 | tf_op jit(solution)/shard_map/all_to_all | solution.py:49
  141.3 0.0 copy-done
  141.3 3.6 %fusion.21 = f32[64,128,64]{1,2,0:T(8,128)} fusion(bf16[64,64,64]{2,1,0:T(8,128)(2,1)S(1)} %copy-done, bf16[128,64,64]{0,1,2:T(8,128)(2,1)} %copy-done.3), kind=kOutput, calls=%fused_computation.28 | convolution fusion | flops 67108864 | bytes 3670016 | tf_op jit(solution)/shard_map/tbj,bkj->tbk/dot_general | solution.py:129
  144.9 2.2 %all-to-all-done.1 = f32[16,1,1024]{2,1,0:T(1,128)S(1)} async-done(((f32[16,1,1024]{2,1,0:T(1,128)}), f32[16,1,1024]{2,1,0:T(1,128)S(1)}, u32[]{:S(2)}, u32[]{:S(2)}) %all-to-all-start.1) | async-done | bytes 65568 | tf_op jit(solution)/shard_map/all_to_all | solution.py:49
  147.1 0.1 reduce_sum.29
  147.1 0.7 broadcast_in_dim.32
  147.8 3.7 %all-to-all-start.2 = ((f32[16,1,1024]{2,1,0:T(1,128)}), f32[16,1,1024]{2,1,0:T(1,128)S(1)}, u32[]{:S(2)}, u32[]{:S(2)}) async-start(f32[16,1,1024]{2,1,0:T(1,128)} %broadcast_in_dim.32), calls=%async_computation.2 | async-start | bytes 131072 | tf_op jit(solution)/shard_map/all_to_all | solution.py:51
  151.6 3.8 %fusion.24 = f32[64,128,64]{1,2,0:T(8,128)} fusion(bf16[64,64,64]{2,1,0:T(8,128)(2,1)S(1)} %copy-done, bf16[128,64,64]{0,1,2:T(8,128)(2,1)} %copy-done.2), kind=kOutput, calls=%fused_computation.31 | convolution fusion | flops 67108864 | bytes 3670016 | tf_op jit(solution)/shard_map/tbk,bkj->tbj/dot_general | solution.py:109
  155.3 2.5 %broadcast_in_dim.17 = f32[128,128,64]{0,2,1:T(8,128)} broadcast(f32[]{:T(128)} %constant.9.clone.1), dimensions={} | broadcast | bytes 4194308 | tf_op jit(solution)/shard_map/broadcast_in_dim | solution.py:131
  157.8 10.6 %scatter_fusion.1 = f32[128,128,64]{0,2,1:T(8,128)} fusion(f32[128,128,64]{0,2,1:T(8,128)} %broadcast_in_dim.17, s32[64]{0:T(128)S(1)} %get-tuple-element.20, f32[64,128,64]{1,2,0:T(8,128)} %fusion.21), kind=kCustom, calls=%fused_computation.1 | custom fusion | flops 524288 | bytes 6291712 | tf_op jit(solution)/shard_map/scatter-add | solution.py:133
  168.4 5.6 %copy.83 = f32[128,8192]{1,0:T(8,128)} copy(f32[128,8192]{0,1:T(8,128)} %bitcast.79) | data formatting | bytes 8388608 | tf_op jit(solution)/shard_map/reshape | solution.py:134
  174.1 7.0 %scatter_fusion = f32[128,16,64]{0,2,1:T(8,128)S(1)} fusion(f32[128,16,64]{0,2,1:T(8,128)S(1)} %broadcast_in_dim.14, s32[64]{0:T(128)S(1)} %get-tuple-element.19, f32[64,128,64]{1,2,0:T(8,128)} %fusion.24), kind=kCustom, calls=%fused_computation | custom fusion | flops 524288 | bytes 6291712 | tf_op jit(solution)/shard_map/scatter-add | solution.py:115
  181.1 0.0 all-to-all-done.2
  181.1 0.2 reduce.2
  181.3 0.7 reshape.66
  182.0 10.9 %fusion.19 = bf16[128,1024]{0,1:T(8,128)(2,1)S(1)} fusion(f32[128,1024]{0,1:T(8,128)S(1)} %bitcast.78, bf16[8192,1024]{1,0:T(8,128)(2,1)} %bitcast.80, bf16[128,8192]{1,0:T(8,128)(2,1)} %param.8), kind=kOutput, calls=%fused_computation.26 | convolution fusion | flops 2147745792 | bytes 19660800 | tf_op jit(solution)/shard_map/dot_general | solution.py:118
  193.0 2.0 convolution_convert_fusion
  195.0 4.1 %copy.88 = bf16[128,8192]{1,0:T(8,128)(2,1)} copy(bf16[128,8192]{0,1:T(8,128)(2,1)} %bitcast.85) | data formatting | bytes 4194304
  199.0 14.0 %fusion.1 = bf16[128,8192]{1,0:T(8,128)(2,1)} fusion(f32[128,8192]{1,0:T(8,128)} %copy.83, bf16[128,1024]{0,1:T(8,128)(2,1)S(1)} %bitcast.87, bf16[8192,1024]{1,0:T(8,128)(2,1)} %bitcast.81), kind=kOutput, calls=%fused_computation.4 | convolution fusion | flops 2149580800 | bytes 23330816 | tf_op jit(solution)/shard_map/dot_general | solution.py:126
  (12 shorter events, 0.1 us)
Async XLA Ops:
  7.2 134.1 %copy-start = (bf16[64,64,64]{2,1,0:T(8,128)(2,1)S(1)}, bf16[64,64,64]{2,1,0:T(8,128)(2,1)}, u32[]{:S(2)}) copy-start(bf16[64,64,64]{2,1,0:T(8,128)(2,1)} %param.13) | copy-start | bytes 1572868
  7.2 65.7 %copy-start.6 = (bf16[128,1024]{1,0:T(8,128)(2,1)S(1)}, bf16[128,1024]{1,0:T(8,128)(2,1)}, u32[]{:S(2)}) copy-start(bf16[128,1024]{1,0:T(8,128)(2,1)} %param.10) | copy-start | bytes 786436
  7.2 65.6 %all-gather.6.cloned.1.call-start = ((), (), s32[]{:S(2)}) async-start(), calls=%async_computation.4 | async-start | bytes 2228224 | tf_op jit(solution)/shard_map/all_gather | solution.py:37
  8.9 173.1 %all-gather.4.cloned.1.call-start = ((), (), s32[]{:S(2)}) async-start(), calls=%async_computation.3 | async-start | bytes 18874368 | tf_op jit(solution)/shard_map/all_gather | solution.py:38
  79.2 4.1 %copy-start.8 = (s32[64,2]{0,1:T(2,128)S(1)}, s32[64,2]{0,1:T(2,128)}, u32[]{:S(2)}) copy-start(s32[64,2]{0,1:T(2,128)} %param.14) | copy-start | bytes 1540
  79.2 4.1 %copy-start.7 = (s32[1,128]{1,0:T(1,128)S(1)}, s32[1,128]{1,0:T(1,128)}, u32[]{:S(2)}) copy-start(s32[1,128]{1,0:T(1,128)} %param.11) | copy-start | bytes 1540
  86.1 1.9 copy-start.5
  88.0 1.9 copy-start.4
  89.2 2.2 %copy-start.3 = (bf16[128,64,64]{0,1,2:T(8,128)(2,1)}, bf16[128,64,64]{0,1,2:T(8,128)(2,1)S(1)}, u32[]{:S(2)}) copy-start(bf16[128,64,64]{0,1,2:T(8,128)(2,1)S(1)} %fusion.13) | copy-start | bytes 3145732
  91.4 1.0 copy-start.2
  134.2 12.8 %all-to-all-start.1 = ((f32[16,1,1024]{2,1,0:T(1,128)}), f32[16,1,1024]{2,1,0:T(1,128)S(1)}, u32[]{:S(2)}, u32[]{:S(2)}) async-start(f32[16,1,1024]{2,1,0:T(1,128)} %bitcast.28), calls=%async_computation.1 | async-start | bytes 131072 | tf_op jit(solution)/shard_map/all_to_all | solution.py:49
  147.8 33.3 %all-to-all-start.2 = ((f32[16,1,1024]{2,1,0:T(1,128)}), f32[16,1,1024]{2,1,0:T(1,128)S(1)}, u32[]{:S(2)}, u32[]{:S(2)}) async-start(f32[16,1,1024]{2,1,0:T(1,128)} %broadcast_in_dim.32), calls=%async_computation.2 | async-start | bytes 131072 | tf_op jit(solution)/shard_map/all_to_all | solution.py:51
  199.0 14.0 %copy-start.1 = (bf16[64,64,64]{2,1,0:T(8,128)(2,1)S(1)}, bf16[64,64,64]{2,1,0:T(8,128)(2,1)}, u32[]{:S(2)}) copy-start(bf16[64,64,64]{2,1,0:T(8,128)(2,1)} %param.13) | copy-start | bytes 1572868
Sparse Core Ops, SparseCore 0:
  11.0 61.7 all-gather.5
  74.7 88.4 all-gather.3

commit v2 on v1

--- a/solution.py
+++ b/solution.py
@@ -28,28 +28,33 @@
     return (row_hot, col_hot)
 
 
-def gather_weight(base_weight):
+def gather_pieces(base_weight):
     rows = base_weight.shape[0]
     pieces = lax.axis_size("x") * lax.axis_size("c")
     width = rows // pieces
     me = lax.axis_index("x") * lax.axis_size("c") + lax.axis_index("c")
     piece = lax.dynamic_slice_in_dim(base_weight, me * width, width, 0)
-    by_shard = lax.all_gather(piece, SHARD, axis=0, tiled=False)
-    whole = lax.all_gather(by_shard, PIECE, axis=1, tiled=True)
-    return whole.reshape(-1, base_weight.shape[1])
+    return lax.all_gather(piece, SHARD, axis=0, tiled=False)
 
 
-def reduce_delta(grad_term):
+def gather_rest(by_shard):
+    whole = lax.all_gather(by_shard, PIECE, axis=1, tiled=True)
+    return whole.reshape(-1, whole.shape[-1])
+
+
+def reduce_delta(grad_term, by_shard):
     n_shard = lax.axis_size(SHARD)
     n_rep = lax.axis_size(REPLICA)
     nb = grad_term.shape[0]
     flat = grad_term.reshape(n_shard, -1)
     mine = lax.all_to_all(flat, SHARD, 0, 0, tiled=False).sum(0)
+    mine, by_shard = lax.optimization_barrier((mine, by_shard))
+    full_weight = gather_rest(by_shard)
     mine = mine.reshape(n_rep, -1)
     part = lax.all_to_all(mine, REPLICA, 0, 0, tiled=False).sum(0)
     spread = jnp.broadcast_to(part[None], (n_rep,) + part.shape)
     whole = lax.all_to_all(spread, REPLICA, 0, 0, tiled=False)
-    return whole.reshape(nb // n_shard, BLK, BLK)
+    return whole.reshape(nb // n_shard, BLK, BLK), full_weight
 
 
 def local(
@@ -66,7 +71,7 @@
     groups = QH // KVH
     row_index = block_list[:, 0]
     col_index = block_list[:, 1]
-    full_weight = gather_weight(base_weight)
+    by_shard = gather_pieces(base_weight)
     row_hot, col_hot = block_tables(block_list)
     picked = jnp.einsum(
         "trk,br->tbk",
@@ -104,7 +109,7 @@
     grad_term = (
         jnp.einsum("tbk,tbj->bkj", picked, chosen, preferred_element_type=jnp.float32) * grad_scale
     )
-    delta_grad = reduce_delta(grad_term)
+    delta_grad, full_weight = reduce_delta(grad_term, by_shard)
 
     block_term = jnp.einsum(
         "tbk,bkj->tbj", picked, delta_values, preferred_element_type=jnp.float32

time: 221 us -> 218 us (0.986)
  waiting for transfers between devices: 66.1 us -> 48.4 us
  blocking collectives: 33.1 us -> 47.2 us
    all_gather x2, waiting for transfers between devices: 63.8 us -> 46.3 us  [the longest x1 41.7 us: gather_rest(): whole = lax.all_gather(by_shard, PIECE, axis=1, tiled=True)]
    all_to_all x1, blocking collectives: 33.1 us -> 47.2 us  [reduce_delta(): mine = lax.all_to_all(flat, SHARD, 0, 0, tiled=False).sum(0)]
  transfers between devices with their start and end apart: 4 -> 4, of which waited for: 2 -> 3; matrix products, arithmetic and copies ran while one was open for 26% -> 26% of each run, Pallas kernels for 0% -> 0%
where the time goes in v2:
time: 218 us; the launch traced here: 217 us
  waiting for transfers between devices  48.4 us (22%)
  blocking collectives  47.2 us (22%)
  matrix products  41.5 us (19%)
  local copies, waits for them, and re-layouts  31.5 us (14%)
  other arithmetic  22 us (10%)
  between operations  14.2 us (7%)
  starting transfers between devices  11.6 us (5%)
    all_to_all x1, blocking collectives, reduce_delta(): mine = lax.all_to_all(flat, SHARD, 0, 0, tiled=False).sum(0)  47.2 us
    all_gather x1, waiting for transfers between devices, gather_rest(): whole = lax.all_gather(by_shard, PIECE, axis=1, tiled=True)  41.7 us
    dot_general x1, matrix products, local(): lax.dot_general(value_grad, full_weight, (((1,), (1,)), ((), ())), prefer...  14 us
    unnamed x22, local copies, waits for them, and re-layouts  12.8 us
    dot_general x1, matrix products, local(): jnp.dot(tokens, full_weight, preferred_element_type=jnp.float32)  10.9 us
    scatter-add x1, other arithmetic, local(): spread_back = jnp.zeros((tok_rows, D // BLK, BLK), jnp.float32).at[:, row...  10.5 us
    all_to_all x1, starting transfers between devices, reduce_delta(): part = lax.all_to_all(mine, REPLICA, 0, 0, tiled=False).sum(0)  7.82 us
    scatter-add x1, other arithmetic, local(): sparse_part = jnp.zeros((tok_rows, KVH * HD // BLK, BLK), jnp.float32).at...  7.04 us
  transfers between devices with their start and end apart: 4, of which 3 were waited for; matrix products, arithmetic and copies ran while one was open for 26% of the time, Pallas kernels for 0%

profile of v2, /device:TPU:1, one launch (start us, length us, event | category | flops | bytes accessed | tf_op | source)
XLA Modules:
  0.0 216.6 jit_solution(7737501125212029642)
XLA Ops:
  7.2 0.0 copy-start
  7.2 0.0 all-gather.6.cloned.1.call-start
  7.2 1.6 constant_dynamic-slice_fusion
  8.9 0.0 all-gather.6.cloned.1.call-update
  8.9 0.0 all-gather.4.cloned.1.call-start
  9.0 4.1 %copy.72 = bf16[128,8192]{0,1:T(8,128)(2,1)} copy(bf16[128,8192]{1,0:T(8,128)(2,1)} %param.8) | data formatting | bytes 4194304 | tf_op args[0]
  13.0 2.2 %copy.100 = bf16[16,8,64,128]{3,2,1,0:T(8,128)(2,1)S(1)} copy(bf16[16,8,64,128]{3,1,2,0:T(8,128)(2,1)} %bitcast.88) | data formatting | bytes 4194304
  15.3 0.0 copy-done.6
  15.3 0.1 fusion.28
  15.4 4.1 %copy.97 = bf16[128,8192]{0,1:T(8,128)(2,1)} copy(bf16[128,8192]{1,0:T(8,128)(2,1)} %param.15) | data formatting | bytes 4194304 | tf_op jit(solution)/shard_map/reshape | solution.py:94
  19.5 1.6 fusion.3
  21.2 0.0 copy-start.8
  21.2 1.1 fusion.39
  22.3 0.0 copy-done.8
  22.3 0.0 copy-start.5
  22.3 0.6 divide_convert_fusion
  22.9 1.0 copy-done.5
  23.9 0.7 fusion.18
  24.6 0.5 fusion.13
  25.1 0.4 copy-done.4
  25.5 1.5 fusion.14
  27.0 0.0 copy-start.3
  27.0 1.0 copy-done.3
  27.9 2.7 %convolution_multiply_fusion = f32[64,64,64]{2,1,0:T(8,128)} fusion(bf16[128,64,64]{0,1,2:T(8,128)(2,1)S(1)} %fusion.13, bf16[128,64,64]{0,1,2:T(8,128)(2,1)S(1)} %fusion.14), kind=kOutput, calls=%fused_computation.17 | convolution fusion | flops 67371008 | bytes 3145728 | tf_op jit(solution)/shard_map/tbk,tbj->bkj/dot_general | solution.py:110
  30.7 3.4 %all_to_all.21 = f32[16,1,16384]{2,1,0:T(1,128)} reshape(f32[64,64,64]{2,1,0:T(8,128)} %convolution_multiply_fusion) | data formatting | bytes 2097152 | tf_op jit(solution)/shard_map/all_to_all | solution.py:50
  34.1 47.2 %all_to_all.25 = f32[16,1,16384]{2,1,0:T(1,128)} all-to-all(f32[16,1,16384]{2,1,0:T(1,128)} %all_to_all.21), channel_id=1, replica_groups=mesh['zl'=2,'x'=4,'c'=2,'zh'=4,'y'=4] {'zh','y'}, dimensions={0} | all-to-all | bytes 2097152 | tf_op jit(solution)/shard_map/all_to_all | solution.py:50
  81.3 2.6 %reduce_sum.28 = f32[16384]{0:T(1024)} reduce(f32[16,1,16384]{2,1,0:T(1,128)} %all_to_all.25, f32[]{:T(128)} %constant.4.clone.1), dimensions={0,1}, to_apply=%region_2.3 | reduce | flops 245760 | bytes 1114116 | tf_op jit(solution)/shard_map/reduce_sum | solution.py:50
  83.9 4.6 %all-gather.6.cloned.1.call-done = bf16[1024,1024]{1,0:T(8,128)(2,1)} async-done(((bf16[64,1024]{1,0:T(8,128)(2,1)}), bf16[1024,1024]{1,0:T(8,128)(2,1)}) %all-gather.6.cloned.1.call-update) | async-done | bytes 2097168 | tf_op jit(solution)/shard_map/all_gather | solution.py:37
  88.5 0.0 all-gather.4.cloned.1.call-update
  88.5 7.8 %all-to-all-start.1 = ((f32[16,1,1024]{2,1,0:T(1,128)}), f32[16,1,1024]{2,1,0:T(1,128)S(1)}, u32[]{:S(2)}, u32[]{:S(2)}) async-start(f32[16,1,1024]{2,1,0:T(1,128)} %bitcast.28), calls=%async_computation.1 | async-start | bytes 131072 | tf_op jit(solution)/shard_map/all_to_all | solution.py:54
  96.4 3.8 %fusion.23 = f32[64,128,64]{1,2,0:T(8,128)} fusion(bf16[64,64,64]{2,1,0:T(8,128)(2,1)S(1)} %copy-done, bf16[128,64,64]{0,1,2:T(8,128)(2,1)} %copy-done.3), kind=kOutput, calls=%fused_computation.30 | convolution fusion | flops 67108864 | bytes 3670016 | tf_op jit(solution)/shard_map/tbk,bkj->tbj/dot_general | solution.py:114
  100.2 2.0 all-to-all-done.1
  102.2 0.1 reduce_sum.29
  102.2 0.7 broadcast_in_dim.32
  102.9 3.7 %all-to-all-start.2 = ((f32[16,1,1024]{2,1,0:T(1,128)}), f32[16,1,1024]{2,1,0:T(1,128)S(1)}, u32[]{:S(2)}, u32[]{:S(2)}) async-start(f32[16,1,1024]{2,1,0:T(1,128)} %broadcast_in_dim.32), calls=%async_computation.2 | async-start | bytes 131072 | tf_op jit(solution)/shard_map/all_to_all | solution.py:56
  106.6 3.7 %fusion.20 = f32[64,128,64]{1,2,0:T(8,128)} fusion(bf16[64,64,64]{2,1,0:T(8,128)(2,1)S(1)} %copy-done, bf16[128,64,64]{0,1,2:T(8,128)(2,1)} %copy-done.2), kind=kOutput, calls=%fused_computation.27 | convolution fusion | flops 67108864 | bytes 3670016 | tf_op jit(solution)/shard_map/tbj,bkj->tbk/dot_general | solution.py:134
  110.3 2.5 %broadcast_in_dim.17 = f32[128,128,64]{0,2,1:T(8,128)} broadcast(f32[]{:T(128)} %constant.4.clone.1), dimensions={} | broadcast | bytes 4194308 | tf_op jit(solution)/shard_map/broadcast_in_dim | solution.py:136
  112.8 10.5 %scatter_fusion.1 = f32[128,128,64]{0,2,1:T(8,128)} fusion(f32[128,128,64]{0,2,1:T(8,128)} %broadcast_in_dim.17, s32[64]{0:T(128)S(1)} %get-tuple-element.22, f32[64,128,64]{1,2,0:T(8,128)} %fusion.20), kind=kCustom, calls=%fused_computation.1 | custom fusion | flops 524288 | bytes 6291712 | tf_op jit(solution)/shard_map/scatter-add | solution.py:138
  123.3 5.7 %copy.86 = f32[128,8192]{1,0:T(8,128)} copy(f32[128,8192]{0,1:T(8,128)} %bitcast.79) | data formatting | bytes 8388608 | tf_op jit(solution)/shard_map/reshape | solution.py:139
  129.0 7.0 %scatter_fusion = f32[128,16,64]{0,2,1:T(8,128)S(1)} fusion(f32[128,16,64]{0,2,1:T(8,128)S(1)} %broadcast_in_dim.16, s32[64]{0:T(128)S(1)} %get-tuple-element.23, f32[64,128,64]{1,2,0:T(8,128)} %fusion.23), kind=kCustom, calls=%fused_computation | custom fusion | flops 524288 | bytes 6291712 | tf_op jit(solution)/shard_map/scatter-add | solution.py:120
  136.1 0.0 all-to-all-done.2
  136.1 0.2 reduce.2
  136.3 0.7 reshape.66
  137.0 41.7 %all-gather.4.cloned.1.call-done = bf16[16,512,1024]{2,1,0:T(8,128)(2,1)} async-done(((bf16[16,64,1024]{2,1,0:T(8,128)(2,1)}), bf16[16,512,1024]{2,1,0:T(8,128)(2,1)}) %all-gather.4.cloned.1.call-update) | async-done | bytes 16777232 | tf_op jit(solution)/shard_map/all_gather | solution.py:41
  178.7 10.9 %fusion.19 = bf16[128,1024]{0,1:T(8,128)(2,1)S(1)} fusion(f32[128,1024]{0,1:T(8,128)S(1)} %bitcast.78, bf16[8192,1024]{1,0:T(8,128)(2,1)} %bitcast.80, bf16[128,8192]{1,0:T(8,128)(2,1)} %param.8), kind=kOutput, calls=%fused_computation.26 | convolution fusion | flops 2147745792 | bytes 19660800 | tf_op jit(solution)/shard_map/dot_general | solution.py:123
  189.6 2.0 convolution_convert_fusion
  191.6 4.1 %copy.88 = bf16[128,8192]{1,0:T(8,128)(2,1)} copy(bf16[128,8192]{0,1:T(8,128)(2,1)} %bitcast.85) | data formatting | bytes 4194304
  195.7 14.0 %fusion.1 = bf16[128,8192]{1,0:T(8,128)(2,1)} fusion(f32[128,8192]{1,0:T(8,128)} %copy.86, bf16[128,1024]{0,1:T(8,128)(2,1)S(1)} %bitcast.87, bf16[8192,1024]{1,0:T(8,128)(2,1)} %bitcast.81), kind=kOutput, calls=%fused_computation.4 | convolution fusion | flops 2149580800 | bytes 23330816 | tf_op jit(solution)/shard_map/dot_general | solution.py:131
  (12 shorter events, 0.1 us)
Async XLA Ops:
  7.2 89.2 %copy-start = (bf16[64,64,64]{2,1,0:T(8,128)(2,1)S(1)}, bf16[64,64,64]{2,1,0:T(8,128)(2,1)}, u32[]{:S(2)}) copy-start(bf16[64,64,64]{2,1,0:T(8,128)(2,1)} %param.13) | copy-start | bytes 1572868
  7.2 81.3 %all-gather.6.cloned.1.call-start = ((), (), s32[]{:S(2)}) async-start(), calls=%async_computation.4 | async-start | bytes 2228224 | tf_op jit(solution)/shard_map/all_gather | solution.py:37
  8.9 169.8 %all-gather.4.cloned.1.call-start = ((), (), s32[]{:S(2)}) async-start(), calls=%async_computation.3 | async-start | bytes 18874368 | tf_op jit(solution)/shard_map/all_gather | solution.py:41
  13.0 2.2 %copy-start.6 = (bf16[128,1024]{1,0:T(8,128)(2,1)S(1)}, bf16[128,1024]{1,0:T(8,128)(2,1)}, u32[]{:S(2)}) copy-start(bf16[128,1024]{1,0:T(8,128)(2,1)} %param.10) | copy-start | bytes 786436
  13.0 2.3 %copy-start.7 = (s32[1,128]{1,0:T(1,128)S(1)}, s32[1,128]{1,0:T(1,128)}, u32[]{:S(2)}) copy-start(s32[1,128]{1,0:T(1,128)} %param.11) | copy-start | bytes 1540
  21.2 1.1 copy-start.8
  22.3 1.6 copy-start.5
  23.9 1.6 copy-start.4
  25.1 1.9 copy-start.2
  27.0 1.0 copy-start.3
  88.5 13.6 %all-to-all-start.1 = ((f32[16,1,1024]{2,1,0:T(1,128)}), f32[16,1,1024]{2,1,0:T(1,128)S(1)}, u32[]{:S(2)}, u32[]{:S(2)}) async-start(f32[16,1,1024]{2,1,0:T(1,128)} %bitcast.28), calls=%async_computation.1 | async-start | bytes 131072 | tf_op jit(solution)/shard_map/all_to_all | solution.py:54
  102.9 33.2 %all-to-all-start.2 = ((f32[16,1,1024]{2,1,0:T(1,128)}), f32[16,1,1024]{2,1,0:T(1,128)S(1)}, u32[]{:S(2)}, u32[]{:S(2)}) async-start(f32[16,1,1024]{2,1,0:T(1,128)} %broadcast_in_dim.32), calls=%async_computation.2 | async-start | bytes 131072 | tf_op jit(solution)/shard_map/all_to_all | solution.py:56
  195.7 14.0 %copy-start.1 = (bf16[64,64,64]{2,1,0:T(8,128)(2,1)S(1)}, bf16[64,64,64]{2,1,0:T(8,128)(2,1)}, u32[]{:S(2)}) copy-start(bf16[64,64,64]{2,1,0:T(8,128)(2,1)} %param.13) | copy-start | bytes 1572868
Sparse Core Ops, SparseCore 0:
  11.0 77.4 all-gather.5
  90.4 88.2 all-gather.3

commit v3 on v2

--- a/solution.py
+++ b/solution.py
@@ -42,19 +42,17 @@
     return whole.reshape(-1, whole.shape[-1])
 
 
-def reduce_delta(grad_term, by_shard):
+def reduce_delta(grad_term):
     n_shard = lax.axis_size(SHARD)
     n_rep = lax.axis_size(REPLICA)
     nb = grad_term.shape[0]
     flat = grad_term.reshape(n_shard, -1)
     mine = lax.all_to_all(flat, SHARD, 0, 0, tiled=False).sum(0)
-    mine, by_shard = lax.optimization_barrier((mine, by_shard))
-    full_weight = gather_rest(by_shard)
     mine = mine.reshape(n_rep, -1)
     part = lax.all_to_all(mine, REPLICA, 0, 0, tiled=False).sum(0)
     spread = jnp.broadcast_to(part[None], (n_rep,) + part.shape)
     whole = lax.all_to_all(spread, REPLICA, 0, 0, tiled=False)
-    return whole.reshape(nb // n_shard, BLK, BLK), full_weight
+    return whole.reshape(nb // n_shard, BLK, BLK)
 
 
 def local(
@@ -109,8 +107,6 @@
     grad_term = (
         jnp.einsum("tbk,tbj->bkj", picked, chosen, preferred_element_type=jnp.float32) * grad_scale
     )
-    delta_grad, full_weight = reduce_delta(grad_term, by_shard)
-
     block_term = jnp.einsum(
         "tbk,bkj->tbj", picked, delta_values, preferred_element_type=jnp.float32
     )
@@ -120,6 +116,18 @@
         .add(block_term)
         .reshape(tok_rows, KVH * HD)
     )
+    back_term = jnp.einsum("tbj,bkj->tbk", chosen, delta_values, preferred_element_type=jnp.float32)
+    spread_back = (
+        jnp.zeros((tok_rows, D // BLK, BLK), jnp.float32)
+        .at[:, row_index]
+        .add(back_term)
+        .reshape(tok_rows, D)
+    )
+    by_shard, grad_term, sparse_part, spread_back = lax.optimization_barrier(
+        (by_shard, grad_term, sparse_part, spread_back)
+    )
+    full_weight = gather_rest(by_shard)
+    delta_grad = reduce_delta(grad_term)
     dense_part = jnp.dot(tokens, full_weight, preferred_element_type=jnp.float32)
     values = (dense_part + sparse_part).astype(jnp.bfloat16)
     value_heads = values.reshape(tok_rows, KVH, HD)
@@ -130,13 +138,6 @@
     )
     dense_back = lax.dot_general(
         value_grad, full_weight, (((1,), (1,)), ((), ())), preferred_element_type=jnp.float32
-    )
-    back_term = jnp.einsum("tbj,bkj->tbk", chosen, delta_values, preferred_element_type=jnp.float32)
-    spread_back = (
-        jnp.zeros((tok_rows, D // BLK, BLK), jnp.float32)
-        .at[:, row_index]
-        .add(back_term)
-        .reshape(tok_rows, D)
     )
     input_grad = (dense_back + spread_back).astype(jnp.bfloat16)
     return (attention, input_grad, delta_grad)

time: 218 us -> 200 us (0.917)
  starting transfers between devices: 11.6 us -> 3.82 us
  waiting for transfers between devices: 48.4 us -> 44.3 us
    all_to_all x1, blocking collectives: 47.2 us -> 33.1 us  [reduce_delta(): mine = lax.all_to_all(flat, SHARD, 0, 0, tiled=False).sum(0)]
    all_to_all x0 -> x1, blocking collectives: none -> 12.4 us  [reduce_delta(): part = lax.all_to_all(mine, REPLICA, 0, 0, tiled=False).sum(0)]
    all_gather x1, waiting for transfers between devices: 41.7 us -> 30 us  [gather_rest(): whole = lax.all_gather(by_shard, PIECE, axis=1, tiled=True)]
    all_gather x1, waiting for transfers between devices: 4.64 us -> 14.3 us  [gather_pieces(): return lax.all_gather(piece, SHARD, axis=0, tiled=False)]
    all_to_all x1 -> x0, starting transfers between devices: 7.82 us -> none  [reduce_delta(): part = lax.all_to_all(mine, REPLICA, 0, 0, tiled=False).sum(0)]
    optimization_barrier x0 -> x1, local copies, waits for them, and re-layouts: none -> 5.86 us  [local(): lax.optimization_barrier((by_shard, grad_term, sparse_part, spread_back))]
    reshape x2 -> x1, local copies, waits for them, and re-layouts: 6.42 us -> 0.74 us  [reduce_delta(): return whole.reshape(nb // n_shard, BLK, BLK)]
    unnamed x22 -> x24, local copies, waits for them, and re-layouts: 12.8 us -> 12.7 us
  transfers between devices with their start and end apart: 4 -> 3, of which waited for: 3 -> 2; matrix products, arithmetic and copies ran while one was open for 26% -> 28% of each run, Pallas kernels for 0% -> 0%
where the time goes in v3:
time: 200 us; the launch traced here: 199 us
  blocking collectives  45.5 us (23%)
  waiting for transfers between devices  44.3 us (22%)
  matrix products  41.2 us (21%)
  local copies, waits for them, and re-layouts  29.5 us (15%)
  other arithmetic  20.2 us (10%)
  between operations  14.2 us (7%)
  starting transfers between devices  3.82 us (2%)
    all_to_all x1, blocking collectives, reduce_delta(): mine = lax.all_to_all(flat, SHARD, 0, 0, tiled=False).sum(0)  33.1 us
    all_gather x1, waiting for transfers between devices, gather_rest(): whole = lax.all_gather(by_shard, PIECE, axis=1, tiled=True)  30 us
    all_gather x1, waiting for transfers between devices, gather_pieces(): return lax.all_gather(piece, SHARD, axis=0, tiled=False)  14.3 us
    dot_general x1, matrix products, local(): lax.dot_general(value_grad, full_weight, (((1,), (1,)), ((), ())), prefer...  14 us
    unnamed x24, local copies, waits for them, and re-layouts  12.7 us
    all_to_all x1, blocking collectives, reduce_delta(): part = lax.all_to_all(mine, REPLICA, 0, 0, tiled=False).sum(0)  12.4 us
    dot_general x1, matrix products, local(): jnp.dot(tokens, full_weight, preferred_element_type=jnp.float32)  11.1 us
    scatter-add x1, other arithmetic, local(): spread_back = jnp.zeros((tok_rows, D // BLK, BLK), jnp.float32).at[:, row...  10.5 us
  transfers between devices with their start and end apart: 3, of which 2 were waited for; matrix products, arithmetic and copies ran while one was open for 28% of the time, Pallas kernels for 0%

profile of v3, /device:TPU:1, one launch (start us, length us, event | category | flops | bytes accessed | tf_op | source)
XLA Modules:
  0.0 198.7 jit_solution(14316450352607943830)
XLA Ops:
  7.2 0.0 copy-start
  7.2 0.0 all-gather.6.cloned.1.call-start
  7.2 1.6 constant_dynamic-slice_fusion
  8.9 0.0 all-gather.6.cloned.1.call-update
  8.9 0.0 all-gather.4.cloned.1.call-start
  9.0 1.0 copy.99
  10.0 0.0 copy-start.7
  10.0 3.7 %copy.100 = bf16[16,8,64,128]{3,2,1,0:T(8,128)(2,1)} copy(bf16[16,8,64,128]{3,1,2,0:T(8,128)(2,1)} %bitcast.88) | data formatting | bytes 4194304
  13.6 0.0 copy-done.7
  13.6 2.5 %copy.97 = bf16[128,8192]{0,1:T(8,128)(2,1)} copy(bf16[128,8192]{1,0:T(8,128)(2,1)S(1)} %copy-done.7) | data formatting | bytes 4194304 | tf_op jit(solution)/shard_map/reshape | solution.py:92
  16.1 4.1 %copy.72 = bf16[128,8192]{0,1:T(8,128)(2,1)} copy(bf16[128,8192]{1,0:T(8,128)(2,1)} %param.8) | data formatting | bytes 4194304 | tf_op args[0]
  20.2 0.0 copy-done.9
  20.2 3.1 %fusion.14 = bf16[128,64,64]{0,1,2:T(8,128)(2,1)S(1)} fusion(bf16[128,128,64]{0,2,1:T(8,128)(2,1)} %bitcast.84, s32[64]{0:T(128)S(1)} %get-tuple-element.29), kind=kOutput, calls=%fused_computation.21 | convolution fusion | flops 134750208 | bytes 3145984 | tf_op jit(solution)/shard_map/trk,br->tbk/dot_general | solution.py:74
  23.3 0.0 copy-done
  23.3 2.6 %fusion.23 = f32[64,128,64]{1,2,0:T(8,128)} fusion(bf16[64,64,64]{2,1,0:T(8,128)(2,1)S(1)} %copy-done, bf16[128,64,64]{0,1,2:T(8,128)(2,1)S(1)} %fusion.14), kind=kOutput, calls=%fused_computation.30 | convolution fusion | flops 67108864 | bytes 3670016 | tf_op jit(solution)/shard_map/tbk,bkj->tbj/dot_general | solution.py:110
  25.9 0.0 copy-start.8
  25.9 7.0 %scatter_fusion = f32[128,16,64]{0,2,1:T(8,128)S(1)} fusion(f32[128,16,64]{0,2,1:T(8,128)S(1)} %broadcast_in_dim.16, s32[64]{0:T(128)S(1)} %get-tuple-element.27, f32[64,128,64]{1,2,0:T(8,128)} %fusion.23), kind=kCustom, calls=%fused_computation | custom fusion | flops 524288 | bytes 6291712 | tf_op jit(solution)/shard_map/scatter-add | solution.py:116
  33.0 0.1 fusion.28
  33.0 3.3 %fusion.3 = f32[8,128,128,8]{2,1,3,0:T(8,128)S(1)} fusion(bf16[128,8,8,128]{3,2,1,0:T(8,128)(2,1)} %bitcast.82, bf16[128,8,128,1]{2,1,0,3:T(8,128)(2,1)S(1)} %bitcast.90), kind=kOutput, calls=%fused_computation.9 | convolution fusion | flops 268435456 | bytes 6553600 | tf_op jit(solution)/shard_map/tgsd,ugd->gstu/dot_general | solution.py:82
  36.3 1.1 fusion.39
  37.4 0.6 divide_convert_fusion
  38.0 0.0 copy-start.2
  38.0 1.0 copy-done.6
  39.1 0.7 fusion.18
  39.8 0.5 fusion.13
  40.3 0.0 copy-start.4
  40.3 2.5 %fusion.20 = f32[64,128,64]{1,2,0:T(8,128)} fusion(bf16[64,64,64]{2,1,0:T(8,128)(2,1)S(1)} %copy-done, bf16[128,64,64]{0,1,2:T(8,128)(2,1)S(1)} %fusion.13), kind=kOutput, calls=%fused_computation.27 | convolution fusion | flops 67108864 | bytes 3670016 | tf_op jit(solution)/shard_map/tbj,bkj->tbk/dot_general | solution.py:119
  42.8 2.5 %broadcast_in_dim.17 = f32[128,128,64]{0,2,1:T(8,128)} broadcast(f32[]{:T(128)} %constant.12.clone.1), dimensions={} | broadcast | bytes 4194308 | tf_op jit(solution)/shard_map/broadcast_in_dim | solution.py:121
  45.3 10.5 %scatter_fusion.1 = f32[128,128,64]{0,2,1:T(8,128)} fusion(f32[128,128,64]{0,2,1:T(8,128)} %broadcast_in_dim.17, s32[64]{0:T(128)S(1)} %get-tuple-element.26, f32[64,128,64]{1,2,0:T(8,128)} %fusion.20), kind=kCustom, calls=%fused_computation.1 | custom fusion | flops 524288 | bytes 6291712 | tf_op jit(solution)/shard_map/scatter-add | solution.py:123
  55.8 2.7 %convolution_multiply_fusion = f32[64,64,64]{2,1,0:T(8,128)} fusion(bf16[128,64,64]{0,1,2:T(8,128)(2,1)S(1)} %copy-done.5, bf16[128,64,64]{0,1,2:T(8,128)(2,1)S(1)} %fusion.14), kind=kOutput, calls=%fused_computation.17 | convolution fusion | flops 67371008 | bytes 3145728 | tf_op jit(solution)/shard_map/tbk,tbj->bkj/dot_general | solution.py:108
  58.6 14.3 %all-gather.6.cloned.1.call-done = bf16[1024,1024]{1,0:T(8,128)(2,1)} async-done(((bf16[64,1024]{1,0:T(8,128)(2,1)}), bf16[1024,1024]{1,0:T(8,128)(2,1)}) %all-gather.6.cloned.1.call-update) | async-done | bytes 2097168 | tf_op jit(solution)/shard_map/all_gather | solution.py:37
  72.8 0.0 all-gather.4.cloned.1.call-update
  72.9 2.8 %all_to_all.21 = f32[16,1,16384]{2,1,0:T(1,128)S(1)} reshape(f32[64,64,64]{2,1,0:T(8,128)} %convolution_multiply_fusion) | data formatting | bytes 2097152 | tf_op jit(solution)/shard_map/all_to_all | solution.py:50
  75.7 33.1 %all_to_all.25 = f32[16,1,16384]{2,1,0:T(1,128)S(1)} all-to-all(f32[16,1,16384]{2,1,0:T(1,128)S(1)} %all_to_all.21), channel_id=1, replica_groups=mesh['zl'=2,'x'=4,'c'=2,'zh'=4,'y'=4] {'zh','y'}, dimensions={0} | all-to-all | bytes 2097152 | tf_op jit(solution)/shard_map/all_to_all | solution.py:50
  108.8 0.7 reduce_sum.28
  109.5 12.4 %all_to_all.26 = f32[16,1,1024]{2,1,0:T(1,128)S(1)} all-to-all(f32[16,1,1024]{2,1,0:T(1,128)S(1)} %bitcast.92), channel_id=1, replica_groups=mesh['zl'=2,'x'=4,'c'=2,'zh'=4,'y'=4] {'zl','x','c'}, dimensions={0} | all-to-all | bytes 131072 | tf_op jit(solution)/shard_map/all_to_all | solution.py:52
  121.9 0.1 reduce_sum.29
  122.0 0.7 broadcast_in_dim.32
  122.7 3.7 %all-to-all-start.2 = ((f32[16,1,1024]{2,1,0:T(1,128)}), f32[16,1,1024]{2,1,0:T(1,128)S(1)}, u32[]{:S(2)}, u32[]{:S(2)}) async-start(f32[16,1,1024]{2,1,0:T(1,128)} %broadcast_in_dim.32), calls=%async_computation.2 | async-start | bytes 131072 | tf_op jit(solution)/shard_map/all_to_all | solution.py:54
  126.4 5.9 %copy.85 = f32[128,8192]{1,0:T(8,128)} copy(f32[128,8192]{0,1:T(8,128)} %bitcast.79) | data formatting | bytes 8388608 | tf_op jit(solution)/shard_map/optimization_barrier | solution.py:126
  132.3 0.0 all-to-all-done.2
  132.3 0.2 reduce.2
  132.4 0.7 reshape.66
  133.2 30.0 %all-gather.4.cloned.1.call-done = bf16[16,512,1024]{2,1,0:T(8,128)(2,1)} async-done(((bf16[16,64,1024]{2,1,0:T(8,128)(2,1)}), bf16[16,512,1024]{2,1,0:T(8,128)(2,1)}) %all-gather.4.cloned.1.call-update) | async-done | bytes 16777232 | tf_op jit(solution)/shard_map/all_gather | solution.py:41
  163.2 11.1 %fusion.19 = bf16[128,1024]{0,1:T(8,128)(2,1)S(1)} fusion(f32[128,1024]{0,1:T(8,128)S(1)} %bitcast.78, bf16[8192,1024]{1,0:T(8,128)(2,1)} %bitcast.80, bf16[128,8192]{1,0:T(8,128)(2,1)} %param.8), kind=kOutput, calls=%fused_computation.26 | convolution fusion | flops 2147745792 | bytes 19660800 | tf_op jit(solution)/shard_map/dot_general | solution.py:131
  174.3 0.7 convolution_convert_fusion
  175.0 2.9 %copy.88 = bf16[128,8192]{1,0:T(8,128)(2,1)} copy(bf16[128,8192]{0,1:T(8,128)(2,1)S(1)} %bitcast.85) | data formatting | bytes 4194304
  177.9 14.0 %fusion.1 = bf16[128,8192]{1,0:T(8,128)(2,1)} fusion(f32[128,8192]{1,0:T(8,128)} %copy.85, bf16[128,1024]{0,1:T(8,128)(2,1)S(1)} %bitcast.87, bf16[8192,1024]{1,0:T(8,128)(2,1)} %bitcast.81), kind=kOutput, calls=%fused_computation.4 | convolution fusion | flops 2149580800 | bytes 23330816 | tf_op jit(solution)/shard_map/dot_general | solution.py:139
  (13 shorter events, 0.1 us)
Async XLA Ops:
  7.2 16.1 %copy-start = (bf16[64,64,64]{2,1,0:T(8,128)(2,1)S(1)}, bf16[64,64,64]{2,1,0:T(8,128)(2,1)}, u32[]{:S(2)}) copy-start(bf16[64,64,64]{2,1,0:T(8,128)(2,1)} %param.13) | copy-start | bytes 1572868
  7.2 65.6 %all-gather.6.cloned.1.call-start = ((), (), s32[]{:S(2)}) async-start(), calls=%async_computation.4 | async-start | bytes 2228224 | tf_op jit(solution)/shard_map/all_gather | solution.py:37
  8.9 154.3 %all-gather.4.cloned.1.call-start = ((), (), s32[]{:S(2)}) async-start(), calls=%async_computation.3 | async-start | bytes 18874368 | tf_op jit(solution)/shard_map/all_gather | solution.py:41
  10.0 3.7 %copy-start.7 = (bf16[128,8192]{1,0:T(8,128)(2,1)S(1)}, bf16[128,8192]{1,0:T(8,128)(2,1)}, u32[]{:S(2)}) copy-start(bf16[128,8192]{1,0:T(8,128)(2,1)} %param.15) | copy-start | bytes 6291460
  16.1 4.1 %copy-start.9 = (s32[64,2]{0,1:T(2,128)S(1)}, s32[64,2]{0,1:T(2,128)}, u32[]{:S(2)}) copy-start(s32[64,2]{0,1:T(2,128)} %param.14) | copy-start | bytes 1540
  25.9 7.1 %copy-start.8 = (s32[1,128]{1,0:T(1,128)S(1)}, s32[1,128]{1,0:T(1,128)}, u32[]{:S(2)}) copy-start(s32[1,128]{1,0:T(1,128)} %param.11) | copy-start | bytes 1540
  37.4 1.7 copy-start.6
  38.0 1.8 copy-start.2
  40.3 2.5 %copy-start.4 = (bf16[128,64,64]{0,1,2:T(8,128)(2,1)}, bf16[128,64,64]{0,1,2:T(8,128)(2,1)S(1)}, u32[]{:S(2)}) copy-start(bf16[128,64,64]{0,1,2:T(8,128)(2,1)S(1)} %fusion.13) | copy-start | bytes 3145732
  45.3 10.5 %copy-start.5 = (bf16[128,64,64]{0,1,2:T(8,128)(2,1)S(1)}, bf16[128,64,64]{0,1,2:T(8,128)(2,1)}, u32[]{:S(2)}) copy-start(bf16[128,64,64]{0,1,2:T(8,128)(2,1)} %copy-done.4) | copy-start | bytes 3145732
  122.7 9.6 %all-to-all-start.2 = ((f32[16,1,1024]{2,1,0:T(1,128)}), f32[16,1,1024]{2,1,0:T(1,128)S(1)}, u32[]{:S(2)}, u32[]{:S(2)}) async-start(f32[16,1,1024]{2,1,0:T(1,128)} %broadcast_in_dim.32), calls=%async_computation.2 | async-start | bytes 131072 | tf_op jit(solution)/shard_map/all_to_all | solution.py:54
  163.2 11.1 %copy-start.3 = (bf16[8,8,128,128]{2,3,1,0:T(8,128)(2,1)S(1)}, bf16[8,8,128,128]{2,3,1,0:T(8,128)(2,1)}, u32[]{:S(2)}) copy-start(bf16[8,8,128,128]{2,3,1,0:T(8,128)(2,1)} %copy-done.2) | copy-start | bytes 6291460
  177.9 14.0 %copy-start.1 = (bf16[64,64,64]{2,1,0:T(8,128)(2,1)S(1)}, bf16[64,64,64]{2,1,0:T(8,128)(2,1)}, u32[]{:S(2)}) copy-start(bf16[64,64,64]{2,1,0:T(8,128)(2,1)} %param.13) | copy-start | bytes 1572868
Sparse Core Ops, SparseCore 0:
  11.0 61.7 all-gather.5
  74.7 88.4 all-gather.3

commit v4 on v3

--- a/solution.py
+++ b/solution.py
@@ -40,6 +40,11 @@
 def gather_rest(by_shard):
     whole = lax.all_gather(by_shard, PIECE, axis=1, tiled=True)
     return whole.reshape(-1, whole.shape[-1])
+
+
+def gather_halves(by_shard):
+    half = by_shard.shape[0] // 2
+    return gather_rest(by_shard[:half]), gather_rest(by_shard[half:])
 
 
 def reduce_delta(grad_term):
@@ -126,9 +131,15 @@
     by_shard, grad_term, sparse_part, spread_back = lax.optimization_barrier(
         (by_shard, grad_term, sparse_part, spread_back)
     )
-    full_weight = gather_rest(by_shard)
+    weight_a, weight_b = gather_halves(by_shard)
+    split = weight_a.shape[0]
     delta_grad = reduce_delta(grad_term)
-    dense_part = jnp.dot(tokens, full_weight, preferred_element_type=jnp.float32)
+    dense_a = jnp.dot(tokens[:, :split], weight_a, preferred_element_type=jnp.float32)
+    back_a = lax.dot_general(
+        value_grad, weight_a, (((1,), (1,)), ((), ())), preferred_element_type=jnp.float32
+    )
+    dense_b = jnp.dot(tokens[:, split:], weight_b, preferred_element_type=jnp.float32)
+    dense_part = dense_a + dense_b
     values = (dense_part + sparse_part).astype(jnp.bfloat16)
     value_heads = values.reshape(tok_rows, KVH, HD)
     attention = (
@@ -136,9 +147,10 @@
         .reshape(tok_rows, QH * HD)
         .astype(jnp.bfloat16)
     )
-    dense_back = lax.dot_general(
-        value_grad, full_weight, (((1,), (1,)), ((), ())), preferred_element_type=jnp.float32
+    back_b = lax.dot_general(
+        value_grad, weight_b, (((1,), (1,)), ((), ())), preferred_element_type=jnp.float32
     )
+    dense_back = jnp.concatenate([back_a, back_b], axis=1)
     input_grad = (dense_back + spread_back).astype(jnp.bfloat16)
     return (attention, input_grad, delta_grad)
 

time: 200 us -> 212 us (1.060)
  waiting for transfers between devices: 44.3 us -> 49.7 us
  local copies, waits for them, and re-layouts: 29.5 us -> 34.8 us
  other arithmetic: 20.2 us -> 25.4 us
  matrix products: 41.2 us -> 37.8 us
    all_gather x1 -> x2, waiting for transfers between devices: 30 us -> 36 us  [gather_rest(): whole = lax.all_gather(by_shard, PIECE, axis=1, tiled=True)]
    convert_element_type x0 -> x1, other arithmetic: none -> 5.29 us  [local(): input_grad = (dense_back + spread_back).astype(jnp.bfloat16)]
    dot_general x2 -> x4, matrix products: 25.1 us -> 20.4 us  [the longest x1 7.82 us: local(): lax.dot_general(value_grad, weight_b, (((1,), (1,)), ((), ())), preferred...]
    slice x0 -> x1, local copies, waits for them, and re-layouts: none -> 3.13 us  [gather_halves(): return (gather_rest(by_shard[:half]), gather_rest(by_shard[half:]))]
    unnamed x24 -> x30, local copies, waits for them, and re-layouts: 12.7 us -> 13.7 us
  transfers between devices with their start and end apart: 3 -> 4, of which waited for: 2 -> 3; matrix products, arithmetic and copies ran while one was open for 28% -> 32% of each run, Pallas kernels for 0% -> 0%
where the time goes in v4:
time: 212 us; the launch traced here: 211 us
  waiting for transfers between devices  49.7 us (23%)
  blocking collectives  45.5 us (21%)
  matrix products  37.8 us (18%)
  local copies, waits for them, and re-layouts  34.8 us (16%)
  other arithmetic  25.4 us (12%)
  between operations  13.9 us (7%)
  starting transfers between devices  4.04 us (2%)
    all_gather x2, waiting for transfers between devices, gather_rest(): whole = lax.all_gather(by_shard, PIECE, axis=1, tiled=True)  36 us
    all_to_all x1, blocking collectives, reduce_delta(): mine = lax.all_to_all(flat, SHARD, 0, 0, tiled=False).sum(0)  33.4 us
    unnamed x30, local copies, waits for them, and re-layouts  13.7 us
    all_gather x1, waiting for transfers between devices, gather_pieces(): return lax.all_gather(piece, SHARD, axis=0, tiled=False)  12.9 us
    all_to_all x1, blocking collectives, reduce_delta(): part = lax.all_to_all(mine, REPLICA, 0, 0, tiled=False).sum(0)  12.1 us
    scatter-add x1, other arithmetic, local(): spread_back = jnp.zeros((tok_rows, D // BLK, BLK), jnp.float32).at[:, row...  10.5 us
    dot_general x1, matrix products, local(): lax.dot_general(value_grad, weight_b, (((1,), (1,)), ((), ())), preferred...  7.82 us
    dot_general x1, matrix products, local(): lax.dot_general(value_grad, weight_a, (((1,), (1,)), ((), ())), preferred...  7.77 us
  transfers between devices with their start and end apart: 4, of which 3 were waited for; matrix products, arithmetic and copies ran while one was open for 32% of the time, Pallas kernels for 0%

profile of v4, /device:TPU:1, one launch (start us, length us, event | category | flops | bytes accessed | tf_op | source)
XLA Modules:
  0.0 211.1 jit_solution(3968502628526506394)
XLA Ops:
  7.2 0.0 copy-start
  7.2 0.0 all-gather.9.cloned.1.call-start
  7.2 1.6 constant_dynamic-slice_fusion
  8.9 0.0 all-gather.9.cloned.1.call-update
  8.9 0.0 all-gather.5.cloned.1.call-start
  9.0 1.0 copy.99
  10.0 3.5 %copy.100 = bf16[16,8,64,128]{3,2,1,0:T(8,128)(2,1)} copy(bf16[16,8,64,128]{3,1,2,0:T(8,128)(2,1)} %bitcast.94) | data formatting | bytes 4194304
  13.5 4.1 %copy.97 = bf16[128,8192]{0,1:T(8,128)(2,1)} copy(bf16[128,8192]{1,0:T(8,128)(2,1)} %param.15) | data formatting | bytes 4194304 | tf_op jit(solution)/shard_map/reshape | solution.py:97
  17.5 4.1 %copy.72 = bf16[128,8192]{0,1:T(8,128)(2,1)} copy(bf16[128,8192]{1,0:T(8,128)(2,1)} %param.8) | data formatting | bytes 4194304 | tf_op args[0]
  21.6 3.1 %fusion.14 = bf16[128,64,64]{0,1,2:T(8,128)(2,1)S(1)} fusion(bf16[128,128,64]{0,2,1:T(8,128)(2,1)} %bitcast.89, s32[64]{0:T(128)S(1)} %get-tuple-element.31), kind=kOutput, calls=%fused_computation.21 | convolution fusion | flops 134750208 | bytes 3145984 | tf_op jit(solution)/shard_map/trk,br->tbk/dot_general | solution.py:79
  24.7 2.6 %fusion.27 = f32[64,128,64]{1,2,0:T(8,128)} fusion(bf16[64,64,64]{2,1,0:T(8,128)(2,1)S(1)} %copy-done, bf16[128,64,64]{0,1,2:T(8,128)(2,1)S(1)} %fusion.14), kind=kOutput, calls=%fused_computation.34 | convolution fusion | flops 67108864 | bytes 3670016 | tf_op jit(solution)/shard_map/tbk,bkj->tbj/dot_general | solution.py:115
  27.3 0.0 copy-start.11
  27.4 7.0 %scatter_fusion = f32[128,16,64]{0,2,1:T(8,128)S(1)} fusion(f32[128,16,64]{0,2,1:T(8,128)S(1)} %broadcast_in_dim.16, s32[64]{0:T(128)S(1)} %get-tuple-element.29, f32[64,128,64]{1,2,0:T(8,128)} %fusion.27), kind=kCustom, calls=%fused_computation | custom fusion | flops 524288 | bytes 6291712 | tf_op jit(solution)/shard_map/scatter-add | solution.py:121
  34.4 0.1 fusion.32
  34.5 3.2 %fusion.3 = f32[8,128,128,8]{2,1,3,0:T(8,128)S(1)} fusion(bf16[128,8,8,128]{3,2,1,0:T(8,128)(2,1)} %bitcast.83, bf16[128,8,128,1]{2,1,0,3:T(8,128)(2,1)S(1)} %bitcast.96), kind=kOutput, calls=%fused_computation.9 | convolution fusion | flops 268435456 | bytes 6553600 | tf_op jit(solution)/shard_map/tgsd,ugd->gstu/dot_general | solution.py:87
  37.8 1.1 fusion.44
  38.9 0.6 divide_convert_fusion
  39.5 1.0 copy-done.8
  40.4 0.7 fusion.20
  41.2 0.5 fusion.13
  41.7 2.5 %fusion.24 = f32[64,128,64]{1,2,0:T(8,128)} fusion(bf16[64,64,64]{2,1,0:T(8,128)(2,1)S(1)} %copy-done, bf16[128,64,64]{0,1,2:T(8,128)(2,1)S(1)} %fusion.13), kind=kOutput, calls=%fused_computation.31 | convolution fusion | flops 67108864 | bytes 3670016 | tf_op jit(solution)/shard_map/tbj,bkj->tbk/dot_general | solution.py:124
  44.2 2.5 %broadcast_in_dim.17 = f32[128,128,64]{0,2,1:T(8,128)} broadcast(f32[]{:T(128)} %constant.12.clone.1), dimensions={} | broadcast | bytes 4194308 | tf_op jit(solution)/shard_map/broadcast_in_dim | solution.py:126
  46.7 10.5 %scatter_fusion.1 = f32[128,128,64]{0,2,1:T(8,128)} fusion(f32[128,128,64]{0,2,1:T(8,128)} %broadcast_in_dim.17, s32[64]{0:T(128)S(1)} %get-tuple-element.28, f32[64,128,64]{1,2,0:T(8,128)} %fusion.24), kind=kCustom, calls=%fused_computation.1 | custom fusion | flops 524288 | bytes 6291712 | tf_op jit(solution)/shard_map/scatter-add | solution.py:128
  57.1 2.7 %convolution_multiply_fusion = f32[64,64,64]{2,1,0:T(8,128)} fusion(bf16[128,64,64]{0,1,2:T(8,128)(2,1)S(1)} %copy-done.5, bf16[128,64,64]{0,1,2:T(8,128)(2,1)S(1)} %fusion.14), kind=kOutput, calls=%fused_computation.17 | convolution fusion | flops 67371008 | bytes 3145728 | tf_op jit(solution)/shard_map/tbk,tbj->bkj/dot_general | solution.py:113
  59.9 12.9 %all-gather.9.cloned.1.call-done = bf16[1024,1024]{1,0:T(8,128)(2,1)} async-done(((bf16[64,1024]{1,0:T(8,128)(2,1)}), bf16[1024,1024]{1,0:T(8,128)(2,1)}) %all-gather.9.cloned.1.call-update) | async-done | bytes 2097168 | tf_op jit(solution)/shard_map/all_gather | solution.py:37
  72.8 3.1 %fusion.43 = (bf16[8,64,1024]{2,1,0:T(8,128)(2,1)}, bf16[8,64,1024]{2,1,0:T(8,128)(2,1)}) fusion(bf16[16,64,1024]{2,1,0:T(8,128)(2,1)} %bitcast.95), kind=kLoop, calls=%fused_computation.56 | loop fusion | bytes 4194304 | tf_op jit(solution)/shard_map/slice | solution.py:47
  75.9 0.0 all-gather.5.cloned.1.call-update
  76.0 0.2 all-gather.7.cloned.1.call-start
  76.2 0.5 all-gather.7.cloned.1.call-update
  76.7 2.7 %all_to_all.21 = f32[16,1,16384]{2,1,0:T(1,128)S(1)} reshape(f32[64,64,64]{2,1,0:T(8,128)} %convolution_multiply_fusion) | data formatting | bytes 2097152 | tf_op jit(solution)/shard_map/all_to_all | solution.py:55
  79.4 33.4 %all_to_all.25 = f32[16,1,16384]{2,1,0:T(1,128)S(1)} all-to-all(f32[16,1,16384]{2,1,0:T(1,128)S(1)} %all_to_all.21), channel_id=1, replica_groups=mesh['zl'=2,'x'=4,'c'=2,'zh'=4,'y'=4] {'zh','y'}, dimensions={0} | all-to-all | bytes 2097152 | tf_op jit(solution)/shard_map/all_to_all | solution.py:55
  112.8 0.7 reduce_sum.28
  113.5 12.1 %all_to_all.26 = f32[16,1,1024]{2,1,0:T(1,128)S(1)} all-to-all(f32[16,1,1024]{2,1,0:T(1,128)S(1)} %bitcast.98), channel_id=1, replica_groups=mesh['zl'=2,'x'=4,'c'=2,'zh'=4,'y'=4] {'zl','x','c'}, dimensions={0} | all-to-all | bytes 131072 | tf_op jit(solution)/shard_map/all_to_all | solution.py:57
  125.6 0.1 reduce_sum.29
  125.6 0.7 broadcast_in_dim.32
  126.3 3.7 %all-to-all-start.2 = ((f32[16,1,1024]{2,1,0:T(1,128)}), f32[16,1,1024]{2,1,0:T(1,128)S(1)}, u32[]{:S(2)}, u32[]{:S(2)}) async-start(f32[16,1,1024]{2,1,0:T(1,128)} %broadcast_in_dim.32), calls=%async_computation.2 | async-start | bytes 131072 | tf_op jit(solution)/shard_map/all_to_all | solution.py:59
  130.0 5.6 %copy.85 = f32[128,8192]{1,0:T(8,128)} copy(f32[128,8192]{0,1:T(8,128)} %bitcast.82) | data formatting | bytes 8388608 | tf_op jit(solution)/shard_map/optimization_barrier | solution.py:131
  135.7 0.3 all-to-all-done.2
  135.9 0.2 reduce.2
  136.1 0.7 reshape.71
  136.8 7.8 %fusion.45 = f32[128,4096]{1,0:T(8,128)} fusion(bf16[128,1024]{0,1:T(8,128)(2,1)S(1)} %bitcast.92, bf16[4096,1024]{1,0:T(8,128)(2,1)} %bitcast.84), kind=kOutput, calls=%fused_computation.58 | convolution fusion | flops 1073741824 | bytes 10747904 | tf_op jit(solution)/shard_map/dot_general | solution.py:138
  144.6 2.4 %fusion.22 = f32[1024,128]{1,0:T(8,128)S(1)} fusion(bf16[4096,1024]{1,0:T(8,128)(2,1)S(1)} %bitcast.85, bf16[128,8192]{1,0:T(8,128)(2,1)S(1)} %copy-done.9), kind=kOutput, calls=%fused_computation.29 | convolution fusion | flops 1073741824 | bytes 9961472 | tf_op jit(solution)/shard_map/dot_general | solution.py:137
  146.9 36.0 %all-gather.7.cloned.1.call-done = bf16[8,512,1024]{2,1,0:T(8,128)(2,1)} async-done(((bf16[8,64,1024]{2,1,0:T(8,128)(2,1)}), bf16[8,512,1024]{2,1,0:T(8,128)(2,1)}) %all-gather.7.cloned.1.call-update) | async-done | bytes 8388624 | tf_op jit(solution)/shard_map/all_gather | solution.py:41
  182.9 7.8 %fusion.46 = f32[128,4096]{1,0:T(8,128)} fusion(bf16[128,1024]{0,1:T(8,128)(2,1)S(1)} %bitcast.93, bf16[4096,1024]{1,0:T(8,128)(2,1)} %bitcast.86), kind=kOutput, calls=%fused_computation.59 | convolution fusion | flops 1073741824 | bytes 10747904 | tf_op jit(solution)/shard_map/dot_general | solution.py:150
  190.8 2.5 %fusion.19 = bf16[128,1024]{0,1:T(8,128)(2,1)S(1)} fusion(f32[128,1024]{0,1:T(8,128)S(1)} %bitcast.81, f32[1024,128]{1,0:T(8,128)S(1)} %fusion.22, bf16[4096,1024]{1,0:T(8,128)(2,1)S(1)} %bitcast.87, bf16[128,8192]{1,0:T(8,128)(2,1)S(1)} %copy-done.10), kind=kOutput, calls=%fused_computation.26 | convolution fusion | flops 1074135040 | bytes 10747904 | tf_op jit(solution)/shard_map/dot_general | solution.py:141
  193.2 2.0 convolution_convert_fusion
  195.3 4.1 %copy.88 = bf16[128,8192]{1,0:T(8,128)(2,1)} copy(bf16[128,8192]{0,1:T(8,128)(2,1)} %bitcast.90) | data formatting | bytes 4194304
  199.3 5.3 %fusion.1 = bf16[128,8192]{1,0:T(8,128)(2,1)} fusion(f32[128,8192]{1,0:T(8,128)} %copy.85, f32[128,4096]{1,0:T(8,128)} %fusion.46, f32[128,4096]{1,0:T(8,128)} %fusion.45), kind=kLoop, calls=%fused_computation.4 | loop fusion | flops 3145728 | bytes 10485760 | tf_op jit(solution)/shard_map/convert_element_type | solution.py:154
  (26 shorter events, 0.1 us)
Async XLA Ops:
  7.2 17.6 %copy-start = (bf16[64,64,64]{2,1,0:T(8,128)(2,1)S(1)}, bf16[64,64,64]{2,1,0:T(8,128)(2,1)}, u32[]{:S(2)}) copy-start(bf16[64,64,64]{2,1,0:T(8,128)(2,1)} %param.13) | copy-start | bytes 1572868
  7.2 65.6 %all-gather.9.cloned.1.call-start = ((), (), s32[]{:S(2)}) async-start(), calls=%async_computation.5 | async-start | bytes 2228224 | tf_op jit(solution)/shard_map/all_gather | solution.py:37
  8.9 127.9 %all-gather.5.cloned.1.call-start = ((), (), s32[]{:S(2)}) async-start(), calls=%async_computation.3 | async-start | bytes 9437184 | tf_op jit(solution)/shard_map/all_gather | solution.py:41
  17.5 4.1 %copy-start.12 = (s32[64,2]{0,1:T(2,128)S(1)}, s32[64,2]{0,1:T(2,128)}, u32[]{:S(2)}) copy-start(s32[64,2]{0,1:T(2,128)} %param.14) | copy-start | bytes 1540
  27.3 7.1 %copy-start.11 = (s32[1,128]{1,0:T(1,128)S(1)}, s32[1,128]{1,0:T(1,128)}, u32[]{:S(2)}) copy-start(s32[1,128]{1,0:T(1,128)} %param.11) | copy-start | bytes 1540
  38.8 1.6 copy-start.8
  39.4 1.7 copy-start.2
  41.7 2.5 %copy-start.4 = (bf16[128,64,64]{0,1,2:T(8,128)(2,1)}, bf16[128,64,64]{0,1,2:T(8,128)(2,1)S(1)}, u32[]{:S(2)}) copy-start(bf16[128,64,64]{0,1,2:T(8,128)(2,1)S(1)} %fusion.13) | copy-start | bytes 3145732
  46.7 10.5 %copy-start.5 = (bf16[128,64,64]{0,1,2:T(8,128)(2,1)S(1)}, bf16[128,64,64]{0,1,2:T(8,128)(2,1)}, u32[]{:S(2)}) copy-start(bf16[128,64,64]{0,1,2:T(8,128)(2,1)} %copy-done.4) | copy-start | bytes 3145732
  76.0 107.0 %all-gather.7.cloned.1.call-start = ((), (), s32[]{:S(2)}) async-start(), calls=%async_computation.4 | async-start | bytes 9437184 | tf_op jit(solution)/shard_map/all_gather | solution.py:41
  126.3 9.6 %all-to-all-start.2 = ((f32[16,1,1024]{2,1,0:T(1,128)}), f32[16,1,1024]{2,1,0:T(1,128)S(1)}, u32[]{:S(2)}, u32[]{:S(2)}) async-start(f32[16,1,1024]{2,1,0:T(1,128)} %broadcast_in_dim.32), calls=%async_computation.2 | async-start | bytes 131072 | tf_op jit(solution)/shard_map/all_to_all | solution.py:59
  136.8 7.8 %copy-start.6 = (bf16[8,512,1024]{2,1,0:T(8,128)(2,1)S(1)}, bf16[8,512,1024]{2,1,0:T(8,128)(2,1)}, u32[]{:S(2)}) copy-start(bf16[8,512,1024]{2,1,0:T(8,128)(2,1)} %all-gather.5.cloned.1.call-done) | copy-start | bytes 25165828
  136.8 7.8 %copy-start.9 = (bf16[128,8192]{1,0:T(8,128)(2,1)S(1)}, bf16[128,8192]{1,0:T(8,128)(2,1)}, u32[]{:S(2)}) copy-start(bf16[128,8192]{1,0:T(8,128)(2,1)} %param.8) | copy-start | bytes 6291460
  182.9 7.8 %copy-start.7 = (bf16[8,512,1024]{2,1,0:T(8,128)(2,1)S(1)}, bf16[8,512,1024]{2,1,0:T(8,128)(2,1)}, u32[]{:S(2)}) copy-start(bf16[8,512,1024]{2,1,0:T(8,128)(2,1)} %all-gather.7.cloned.1.call-done) | copy-start | bytes 25165828
  182.9 7.8 %copy-start.10 = (bf16[128,8192]{1,0:T(8,128)(2,1)S(1)}, bf16[128,8192]{1,0:T(8,128)(2,1)}, u32[]{:S(2)}) copy-start(bf16[128,8192]{1,0:T(8,128)(2,1)} %param.8) | copy-start | bytes 6291460
  190.8 2.5 %copy-start.3 = (bf16[8,8,128,128]{2,3,1,0:T(8,128)(2,1)S(1)}, bf16[8,8,128,128]{2,3,1,0:T(8,128)(2,1)}, u32[]{:S(2)}) copy-start(bf16[8,8,128,128]{2,3,1,0:T(8,128)(2,1)} %copy-done.2) | copy-start | bytes 6291460
  199.3 5.3 %copy-start.1 = (bf16[64,64,64]{2,1,0:T(8,128)(2,1)S(1)}, bf16[64,64,64]{2,1,0:T(8,128)(2,1)}, u32[]{:S(2)}) copy-start(bf16[64,64,64]{2,1,0:T(8,128)(2,1)} %param.13) | copy-start | bytes 1572868
Sparse Core Ops, SparseCore 0:
  11.0 61.7 all-gather.8
  76.1 52.5 all-gather.4
  130.5 52.3 all-gather.6

commit v5 on v3

--- a/solution.py
+++ b/solution.py
@@ -3,6 +3,8 @@
 import jax
 import jax.numpy as jnp
 from jax import lax
+from jax.experimental import pallas as pl
+from jax.experimental.pallas import tpu as pltpu
 from jax.sharding import Mesh
 from jax.sharding import PartitionSpec as P
 
@@ -40,6 +42,58 @@
 def gather_rest(by_shard):
     whole = lax.all_gather(by_shard, PIECE, axis=1, tiled=True)
     return whole.reshape(-1, whole.shape[-1])
+
+
+def tail_kernel(tok_ref, w_ref, vg_ref, sb_ref, sp_ref, val_ref, ig_ref, acc_ref):
+    k = pl.program_id(0)
+
+    @pl.when(k == 0)
+    def _():
+        acc_ref[...] = sp_ref[...]
+
+    w = w_ref[...]
+    acc_ref[...] += jnp.dot(tok_ref[...], w, preferred_element_type=jnp.float32)
+    back = lax.dot_general(
+        vg_ref[...], w, (((1,), (1,)), ((), ())), preferred_element_type=jnp.float32
+    )
+    ig_ref[...] = (back + sb_ref[...]).astype(ig_ref.dtype)
+
+    @pl.when(k == pl.num_programs(0) - 1)
+    def _():
+        val_ref[...] = acc_ref[...].astype(val_ref.dtype)
+
+
+def dense_tail(tokens, full_weight, value_grad, spread_back, sparse_part):
+    rows, depth = tokens.shape
+    width = full_weight.shape[1]
+    tile = 512
+    steps = depth // tile
+    return pl.pallas_call(
+        tail_kernel,
+        grid=(steps,),
+        in_specs=[
+            pl.BlockSpec((rows, tile), lambda k: (0, k)),
+            pl.BlockSpec((tile, width), lambda k: (k, 0)),
+            pl.BlockSpec((rows, width), lambda k: (0, 0)),
+            pl.BlockSpec((rows, tile), lambda k: (0, k)),
+            pl.BlockSpec((rows, width), lambda k: (0, 0)),
+        ],
+        out_specs=[
+            pl.BlockSpec((rows, width), lambda k: (0, 0)),
+            pl.BlockSpec((rows, tile), lambda k: (0, k)),
+        ],
+        out_shape=[
+            jax.ShapeDtypeStruct((rows, width), jnp.bfloat16),
+            jax.ShapeDtypeStruct((rows, depth), jnp.bfloat16),
+        ],
+        scratch_shapes=[pltpu.VMEM((rows, width), jnp.float32)],
+        compiler_params=pltpu.CompilerParams(dimension_semantics=("arbitrary",)),
+        cost_estimate=pl.CostEstimate(
+            flops=4 * rows * depth * width,
+            bytes_accessed=2 * depth * width + 8 * rows * depth + 10 * rows * width,
+            transcendentals=0,
+        ),
+    )(tokens, full_weight, value_grad, spread_back, sparse_part)
 
 
 def reduce_delta(grad_term):
@@ -128,18 +182,13 @@
     )
     full_weight = gather_rest(by_shard)
     delta_grad = reduce_delta(grad_term)
-    dense_part = jnp.dot(tokens, full_weight, preferred_element_type=jnp.float32)
-    values = (dense_part + sparse_part).astype(jnp.bfloat16)
+    values, input_grad = dense_tail(tokens, full_weight, value_grad, spread_back, sparse_part)
     value_heads = values.reshape(tok_rows, KVH, HD)
     attention = (
         jnp.einsum("gstu,ugd->tgsd", attn_probs, value_heads, preferred_element_type=jnp.float32)
         .reshape(tok_rows, QH * HD)
         .astype(jnp.bfloat16)
     )
-    dense_back = lax.dot_general(
-        value_grad, full_weight, (((1,), (1,)), ((), ())), preferred_element_type=jnp.float32
-    )
-    input_grad = (dense_back + spread_back).astype(jnp.bfloat16)
     return (attention, input_grad, delta_grad)
 
 

time: 200 us -> 198 us (0.990)
  matrix products: 41.2 us -> 17.4 us
  Pallas kernels: 0 us -> 19 us
  local copies, waits for them, and re-layouts: 29.5 us -> 33.5 us
    dot_general x2 -> x0, matrix products: 25.1 us -> none  [the longest x1 14 us: local(): lax.dot_general(value_grad, full_weight, (((1,), (1,)), ((), ())), prefer...]
    pallas_call x0 -> x1, Pallas kernels: none -> 19 us  [dense_tail(): pl.pallas_call(tail_kernel, grid=(steps,), in_specs=[pl.BlockSpec((rows,...]
    optimization_barrier x1 -> x2, local copies, waits for them, and re-layouts: 5.86 us -> 6.67 us  [local(): lax.optimization_barrier((by_shard, grad_term, sparse_part, spread_back))]
  transfers between devices with their start and end apart: 3 -> 3, of which waited for: 2 -> 2; matrix products, arithmetic and copies ran while one was open for 28% -> 30% of each run, Pallas kernels for 0% -> 0%
where the time goes in v5:
time: 198 us; the launch traced here: 196 us
  blocking collectives  45.5 us (23%)
  waiting for transfers between devices  42.6 us (22%)
  local copies, waits for them, and re-layouts  33.5 us (17%)
  other arithmetic  20.3 us (10%)
  Pallas kernels  19 us (10%)
  matrix products  17.4 us (9%)
  between operations  14.2 us (7%)
  starting transfers between devices  3.81 us (2%)
    all_to_all x1, blocking collectives, reduce_delta(): mine = lax.all_to_all(flat, SHARD, 0, 0, tiled=False).sum(0)  33.4 us
    all_gather x1, waiting for transfers between devices, gather_rest(): whole = lax.all_gather(by_shard, PIECE, axis=1, tiled=True)  28.4 us
    pallas_call x1, Pallas kernels, dense_tail(): pl.pallas_call(tail_kernel, grid=(steps,), in_specs=[pl.BlockSpec((rows,...  19 us
    all_gather x1, waiting for transfers between devices, gather_pieces(): return lax.all_gather(piece, SHARD, axis=0, tiled=False)  14.2 us
    unnamed x24, local copies, waits for them, and re-layouts  12.2 us
    all_to_all x1, blocking collectives, reduce_delta(): part = lax.all_to_all(mine, REPLICA, 0, 0, tiled=False).sum(0)  12.1 us
    scatter-add x1, other arithmetic, local(): spread_back = jnp.zeros((tok_rows, D // BLK, BLK), jnp.float32).at[:, row...  10.6 us
    scatter-add x1, other arithmetic, local(): sparse_part = jnp.zeros((tok_rows, KVH * HD // BLK, BLK), jnp.float32).at...  7.04 us
  transfers between devices with their start and end apart: 3, of which 2 were waited for; matrix products, arithmetic and copies ran while one was open for 30% of the time, Pallas kernels for 0%

profile of v5, /device:TPU:1, one launch (start us, length us, event | category | flops | bytes accessed | tf_op | source)
XLA Modules:
  0.0 196.4 jit_solution(17130478012400075991)
XLA Ops:
  7.2 0.0 copy-start
  7.2 0.0 all-gather.6.cloned.1.call-start
  7.2 1.6 constant_dynamic-slice_fusion
  8.9 0.0 all-gather.6.cloned.1.call-update
  8.9 0.0 all-gather.4.cloned.1.call-start
  9.0 1.0 copy.116
  10.0 3.5 %copy.117 = bf16[16,8,64,128]{3,2,1,0:T(8,128)(2,1)} copy(bf16[16,8,64,128]{3,1,2,0:T(8,128)(2,1)} %bitcast.77) | data formatting | bytes 4194304
  13.5 4.2 %copy.112 = bf16[128,8192]{0,1:T(8,128)(2,1)} copy(bf16[128,8192]{1,0:T(8,128)(2,1)} %param.15) | data formatting | bytes 4194304 | tf_op jit(solution)/shard_map/reshape | solution.py:146
  17.7 2.5 %copy.84 = bf16[128,8192]{0,1:T(8,128)(2,1)} copy(bf16[128,8192]{1,0:T(8,128)(2,1)S(1)} %copy-done.6) | data formatting | bytes 4194304 | tf_op args[0]
  20.1 0.0 copy-done.9
  20.2 3.1 %fusion.13 = bf16[128,64,64]{0,1,2:T(8,128)(2,1)S(1)} fusion(bf16[128,128,64]{0,2,1:T(8,128)(2,1)} %bitcast.73, s32[64]{0:T(128)S(1)} %get-tuple-element.33), kind=kOutput, calls=%fused_computation.19 | convolution fusion | flops 134750208 | bytes 3145984 | tf_op jit(solution)/shard_map/trk,br->tbk/dot_general | solution.py:128
  23.2 0.0 copy-done
  23.3 2.6 %fusion.20 = f32[64,128,64]{1,2,0:T(8,128)} fusion(bf16[64,64,64]{2,1,0:T(8,128)(2,1)S(1)} %copy-done, bf16[128,64,64]{0,1,2:T(8,128)(2,1)S(1)} %fusion.13), kind=kOutput, calls=%fused_computation.25 | convolution fusion | flops 67108864 | bytes 3670016 | tf_op jit(solution)/shard_map/tbk,bkj->tbj/dot_general | solution.py:164
  25.9 0.0 copy-start.8
  25.9 7.0 %scatter_fusion = f32[128,16,64]{0,2,1:T(8,128)S(1)} fusion(f32[128,16,64]{0,2,1:T(8,128)S(1)} %broadcast_in_dim.16, s32[64]{0:T(128)S(1)} %get-tuple-element.31, f32[64,128,64]{1,2,0:T(8,128)} %fusion.20), kind=kCustom, calls=%fused_computation | custom fusion | flops 524288 | bytes 6291712 | tf_op jit(solution)/shard_map/scatter-add | solution.py:170
  33.0 0.1 fusion.25
  33.1 3.3 %fusion.2 = f32[8,128,128,8]{2,1,3,0:T(8,128)S(1)} fusion(bf16[128,8,8,128]{3,2,1,0:T(8,128)(2,1)} %bitcast.71, bf16[128,8,128,1]{2,1,0,3:T(8,128)(2,1)S(1)} %bitcast.79), kind=kOutput, calls=%fused_computation.7 | convolution fusion | flops 268435456 | bytes 6553600 | tf_op jit(solution)/shard_map/tgsd,ugd->gstu/dot_general | solution.py:136
  36.3 1.1 fusion.36
  37.4 0.0 copy-start.7
  37.4 0.6 divide_convert_fusion
  38.0 1.0 copy-done.7
  39.1 0.7 fusion.16
  39.8 0.5 fusion.12
  40.3 0.0 copy-start.4
  40.3 2.5 %fusion.17 = f32[64,128,64]{1,2,0:T(8,128)} fusion(bf16[64,64,64]{2,1,0:T(8,128)(2,1)S(1)} %copy-done, bf16[128,64,64]{0,1,2:T(8,128)(2,1)S(1)} %fusion.12), kind=kOutput, calls=%fused_computation.22 | convolution fusion | flops 67108864 | bytes 3670016 | tf_op jit(solution)/shard_map/tbj,bkj->tbk/dot_general | solution.py:173
  42.8 2.5 %broadcast_in_dim.17 = f32[128,128,64]{0,2,1:T(8,128)} broadcast(f32[]{:T(128)} %constant.12.clone.1), dimensions={} | broadcast | bytes 4194308 | tf_op jit(solution)/shard_map/broadcast_in_dim | solution.py:175
  45.3 10.6 %scatter_fusion.1 = f32[128,128,64]{0,2,1:T(8,128)} fusion(f32[128,128,64]{0,2,1:T(8,128)} %broadcast_in_dim.17, s32[64]{0:T(128)S(1)} %get-tuple-element.30, f32[64,128,64]{1,2,0:T(8,128)} %fusion.17), kind=kCustom, calls=%fused_computation.1 | custom fusion | flops 524288 | bytes 6291712 | tf_op jit(solution)/shard_map/scatter-add | solution.py:177
  55.9 2.7 %convolution_multiply_fusion = f32[64,64,64]{2,1,0:T(8,128)} fusion(bf16[128,64,64]{0,1,2:T(8,128)(2,1)S(1)} %copy-done.5, bf16[128,64,64]{0,1,2:T(8,128)(2,1)S(1)} %fusion.13), kind=kOutput, calls=%fused_computation.15 | convolution fusion | flops 67371008 | bytes 3145728 | tf_op jit(solution)/shard_map/tbk,tbj->bkj/dot_general | solution.py:162
  58.6 14.2 %all-gather.6.cloned.1.call-done = bf16[1024,1024]{1,0:T(8,128)(2,1)} async-done(((bf16[64,1024]{1,0:T(8,128)(2,1)}), bf16[1024,1024]{1,0:T(8,128)(2,1)}) %all-gather.6.cloned.1.call-update) | async-done | bytes 2097168 | tf_op jit(solution)/shard_map/all_gather | solution.py:39
  72.8 0.0 all-gather.4.cloned.1.call-update
  72.8 2.8 %all_to_all.21 = f32[16,1,16384]{2,1,0:T(1,128)S(1)} reshape(f32[64,64,64]{2,1,0:T(8,128)} %convolution_multiply_fusion) | data formatting | bytes 2097152 | tf_op jit(solution)/shard_map/all_to_all | solution.py:104
  75.7 33.4 %all_to_all.25 = f32[16,1,16384]{2,1,0:T(1,128)S(1)} all-to-all(f32[16,1,16384]{2,1,0:T(1,128)S(1)} %all_to_all.21), channel_id=1, replica_groups=mesh['zl'=2,'x'=4,'c'=2,'zh'=4,'y'=4] {'zh','y'}, dimensions={0} | all-to-all | bytes 2097152 | tf_op jit(solution)/shard_map/all_to_all | solution.py:104
  109.1 0.7 reduce_sum.28
  109.8 12.1 %all_to_all.26 = f32[16,1,1024]{2,1,0:T(1,128)S(1)} all-to-all(f32[16,1,1024]{2,1,0:T(1,128)S(1)} %bitcast.81), channel_id=1, replica_groups=mesh['zl'=2,'x'=4,'c'=2,'zh'=4,'y'=4] {'zl','x','c'}, dimensions={0} | all-to-all | bytes 131072 | tf_op jit(solution)/shard_map/all_to_all | solution.py:106
  121.9 0.1 reduce_sum.29
  121.9 0.7 broadcast_in_dim.32
  122.6 3.7 %all-to-all-start.2 = ((f32[16,1,1024]{2,1,0:T(1,128)}), f32[16,1,1024]{2,1,0:T(1,128)S(1)}, u32[]{:S(2)}, u32[]{:S(2)}) async-start(f32[16,1,1024]{2,1,0:T(1,128)} %broadcast_in_dim.32), calls=%async_computation.2 | async-start | bytes 131072 | tf_op jit(solution)/shard_map/all_to_all | solution.py:108
  126.3 0.9 copy.113.vg_ref
  127.2 1.0 copy.98.sp_ref
  128.2 5.7 %copy.97.sb_ref = f32[128,8192]{1,0:T(8,128)} copy(f32[128,8192]{0,1:T(8,128)} %bitcast.69) | data formatting | bytes 8388608 | tf_op jit(solution)/shard_map/optimization_barrier | solution.py:180
  133.9 0.0 all-to-all-done.2
  133.9 0.2 reduce.2
  134.0 0.7 reshape.66
  134.8 28.4 %all-gather.4.cloned.1.call-done = bf16[16,512,1024]{2,1,0:T(8,128)(2,1)} async-done(((bf16[16,64,1024]{2,1,0:T(8,128)(2,1)}), bf16[16,512,1024]{2,1,0:T(8,128)(2,1)}) %all-gather.4.cloned.1.call-update) | async-done | bytes 16777232 | tf_op jit(solution)/shard_map/all_gather | solution.py:43
  163.2 19.0 %shard_map.103 = (bf16[128,1024]{1,0:T(8,128)(2,1)}, bf16[128,8192]{1,0:T(8,128)(2,1)}) custom-call(bf16[128,8192]{1,0:T(8,128)(2,1)} %tok_ref.1, bf16[8192,1024]{1,0:T(8,128)(2,1)} %bitcast.70, bf16[128,1024]{1,0:T(8,128)(2,1)} %copy.113.vg_ref, f32[128,8192]{1,0:T(8,128)} %copy.97.sb_ref, f32[128,1024]{1,0:T(8,128)} %copy.98.sp_ref), custom_call_target="tpu_custom_call" | custom-call | flops 4294967296 | bytes 26476544 | tf_op jit(solution)/shard_map/pallas_call | solution.py:71
  182.2 1.1 copy.114
  183.3 2.0 %convolution_convert_fusion = bf16[8,128,8,128]{3,1,2,0:T(8,128)(2,1)} fusion(bf16[128,8,128,1]{0,2,3,1:T(8,128)(2,1)S(1)} %bitcast.80, bf16[8,8,128,128]{2,3,1,0:T(8,128)(2,1)S(1)} %copy-done.3), kind=kOutput, calls=%fused_computation.14 | convolution fusion | flops 269484032 | bytes 4456448 | tf_op jit(solution)/shard_map/gstu,ugd->tgsd/dot_general | solution.py:188
  185.4 4.2 %copy.103 = bf16[128,8192]{1,0:T(8,128)(2,1)} copy(bf16[128,8192]{0,1:T(8,128)(2,1)} %bitcast.74) | data formatting | bytes 4194304
  (15 shorter events, 0.1 us)
Async XLA Ops:
  7.2 16.1 %copy-start = (bf16[64,64,64]{2,1,0:T(8,128)(2,1)S(1)}, bf16[64,64,64]{2,1,0:T(8,128)(2,1)}, u32[]{:S(2)}) copy-start(bf16[64,64,64]{2,1,0:T(8,128)(2,1)} %param.13) | copy-start | bytes 1572868
  7.2 65.6 %all-gather.6.cloned.1.call-start = ((), (), s32[]{:S(2)}) async-start(), calls=%async_computation.4 | async-start | bytes 2228224 | tf_op jit(solution)/shard_map/all_gather | solution.py:39
  8.9 154.3 %all-gather.4.cloned.1.call-start = ((), (), s32[]{:S(2)}) async-start(), calls=%async_computation.3 | async-start | bytes 18874368 | tf_op jit(solution)/shard_map/all_gather | solution.py:43
  13.5 4.2 %copy-start.6 = (bf16[128,8192]{1,0:T(8,128)(2,1)S(1)}, bf16[128,8192]{1,0:T(8,128)(2,1)}, u32[]{:S(2)}) copy-start(bf16[128,8192]{1,0:T(8,128)(2,1)} %tok_ref.1) | copy-start | bytes 6291460
  17.7 2.5 %copy-start.9 = (s32[64,2]{0,1:T(2,128)S(1)}, s32[64,2]{0,1:T(2,128)}, u32[]{:S(2)}) copy-start(s32[64,2]{0,1:T(2,128)} %param.14) | copy-start | bytes 1540
  25.9 7.1 %copy-start.8 = (s32[1,128]{1,0:T(1,128)S(1)}, s32[1,128]{1,0:T(1,128)}, u32[]{:S(2)}) copy-start(s32[1,128]{1,0:T(1,128)} %param.11) | copy-start | bytes 1540
  37.4 1.7 copy-start.7
  38.0 1.8 copy-start.2
  40.3 2.5 %copy-start.4 = (bf16[128,64,64]{0,1,2:T(8,128)(2,1)}, bf16[128,64,64]{0,1,2:T(8,128)(2,1)S(1)}, u32[]{:S(2)}) copy-start(bf16[128,64,64]{0,1,2:T(8,128)(2,1)S(1)} %fusion.12) | copy-start | bytes 3145732
  45.3 10.6 %copy-start.5 = (bf16[128,64,64]{0,1,2:T(8,128)(2,1)S(1)}, bf16[128,64,64]{0,1,2:T(8,128)(2,1)}, u32[]{:S(2)}) copy-start(bf16[128,64,64]{0,1,2:T(8,128)(2,1)} %copy-done.4) | copy-start | bytes 3145732
  122.6 11.3 %all-to-all-start.2 = ((f32[16,1,1024]{2,1,0:T(1,128)}), f32[16,1,1024]{2,1,0:T(1,128)S(1)}, u32[]{:S(2)}, u32[]{:S(2)}) async-start(f32[16,1,1024]{2,1,0:T(1,128)} %broadcast_in_dim.32), calls=%async_computation.2 | async-start | bytes 131072 | tf_op jit(solution)/shard_map/all_to_all | solution.py:108
  163.2 20.1 %copy-start.3 = (bf16[8,8,128,128]{2,3,1,0:T(8,128)(2,1)S(1)}, bf16[8,8,128,128]{2,3,1,0:T(8,128)(2,1)}, u32[]{:S(2)}) copy-start(bf16[8,8,128,128]{2,3,1,0:T(8,128)(2,1)} %copy-done.2) | copy-start | bytes 6291460
  185.4 4.2 %copy-start.1 = (bf16[64,64,64]{2,1,0:T(8,128)(2,1)S(1)}, bf16[64,64,64]{2,1,0:T(8,128)(2,1)}, u32[]{:S(2)}) copy-start(bf16[64,64,64]{2,1,0:T(8,128)(2,1)} %param.13) | copy-start | bytes 1572868
Sparse Core Ops, SparseCore 0:
  11.0 61.7 all-gather.5
  74.6 88.4 all-gather.3

commit v6 on v5

--- a/solution.py
+++ b/solution.py
@@ -66,7 +66,7 @@
 def dense_tail(tokens, full_weight, value_grad, spread_back, sparse_part):
     rows, depth = tokens.shape
     width = full_weight.shape[1]
-    tile = 512
+    tile = 1024
     steps = depth // tile
     return pl.pallas_call(
         tail_kernel,

time: 198 us -> 194 us (0.980)
  Pallas kernels: 19 us -> 15.3 us
    pallas_call x1, Pallas kernels: 19 us -> 15.3 us  [dense_tail(): pl.pallas_call(tail_kernel, grid=(steps,), in_specs=[pl.BlockSpec((rows,...]
where the time goes in v6:
time: 194 us; the launch traced here: 193 us
  blocking collectives  45.3 us (23%)
  waiting for transfers between devices  42.9 us (22%)
  local copies, waits for them, and re-layouts  33.5 us (17%)
  other arithmetic  20.2 us (10%)
  matrix products  17.4 us (9%)
  Pallas kernels  15.3 us (8%)
  between operations  14.2 us (7%)
  starting transfers between devices  3.81 us (2%)
    all_to_all x1, blocking collectives, reduce_delta(): mine = lax.all_to_all(flat, SHARD, 0, 0, tiled=False).sum(0)  33.2 us
    all_gather x1, waiting for transfers between devices, gather_rest(): whole = lax.all_gather(by_shard, PIECE, axis=1, tiled=True)  28.4 us
    pallas_call x1, Pallas kernels, dense_tail(): pl.pallas_call(tail_kernel, grid=(steps,), in_specs=[pl.BlockSpec((rows,...  15.3 us
    all_gather x1, waiting for transfers between devices, gather_pieces(): return lax.all_gather(piece, SHARD, axis=0, tiled=False)  14.5 us
    unnamed x24, local copies, waits for them, and re-layouts  12.2 us
    all_to_all x1, blocking collectives, reduce_delta(): part = lax.all_to_all(mine, REPLICA, 0, 0, tiled=False).sum(0)  12.1 us
    scatter-add x1, other arithmetic, local(): spread_back = jnp.zeros((tok_rows, D // BLK, BLK), jnp.float32).at[:, row...  10.5 us
    scatter-add x1, other arithmetic, local(): sparse_part = jnp.zeros((tok_rows, KVH * HD // BLK, BLK), jnp.float32).at...  7.04 us
  transfers between devices with their start and end apart: 3, of which 2 were waited for; matrix products, arithmetic and copies ran while one was open for 30% of the time, Pallas kernels for 0%

profile of v6, /device:TPU:1, one launch (start us, length us, event | category | flops | bytes accessed | tf_op | source)
XLA Modules:
  0.0 192.6 jit_solution(13325748741667443714)
XLA Ops:
  7.2 0.0 copy-start
  7.2 0.0 all-gather.6.cloned.1.call-start
  7.2 1.6 constant_dynamic-slice_fusion
  8.9 0.0 all-gather.6.cloned.1.call-update
  8.9 0.0 all-gather.4.cloned.1.call-start
  9.0 1.0 copy.116
  10.0 3.5 %copy.117 = bf16[16,8,64,128]{3,2,1,0:T(8,128)(2,1)} copy(bf16[16,8,64,128]{3,1,2,0:T(8,128)(2,1)} %bitcast.77) | data formatting | bytes 4194304
  13.5 4.2 %copy.112 = bf16[128,8192]{0,1:T(8,128)(2,1)} copy(bf16[128,8192]{1,0:T(8,128)(2,1)} %param.15) | data formatting | bytes 4194304 | tf_op jit(solution)/shard_map/reshape | solution.py:146
  17.7 2.5 %copy.84 = bf16[128,8192]{0,1:T(8,128)(2,1)} copy(bf16[128,8192]{1,0:T(8,128)(2,1)S(1)} %copy-done.6) | data formatting | bytes 4194304 | tf_op args[0]
  20.1 0.0 copy-done.9
  20.2 3.1 %fusion.13 = bf16[128,64,64]{0,1,2:T(8,128)(2,1)S(1)} fusion(bf16[128,128,64]{0,2,1:T(8,128)(2,1)} %bitcast.73, s32[64]{0:T(128)S(1)} %get-tuple-element.33), kind=kOutput, calls=%fused_computation.19 | convolution fusion | flops 134750208 | bytes 3145984 | tf_op jit(solution)/shard_map/trk,br->tbk/dot_general | solution.py:128
  23.2 0.0 copy-done
  23.3 2.6 %fusion.20 = f32[64,128,64]{1,2,0:T(8,128)} fusion(bf16[64,64,64]{2,1,0:T(8,128)(2,1)S(1)} %copy-done, bf16[128,64,64]{0,1,2:T(8,128)(2,1)S(1)} %fusion.13), kind=kOutput, calls=%fused_computation.25 | convolution fusion | flops 67108864 | bytes 3670016 | tf_op jit(solution)/shard_map/tbk,bkj->tbj/dot_general | solution.py:164
  25.9 0.0 copy-start.8
  25.9 7.0 %scatter_fusion = f32[128,16,64]{0,2,1:T(8,128)S(1)} fusion(f32[128,16,64]{0,2,1:T(8,128)S(1)} %broadcast_in_dim.16, s32[64]{0:T(128)S(1)} %get-tuple-element.31, f32[64,128,64]{1,2,0:T(8,128)} %fusion.20), kind=kCustom, calls=%fused_computation | custom fusion | flops 524288 | bytes 6291712 | tf_op jit(solution)/shard_map/scatter-add | solution.py:170
  33.0 0.1 fusion.25
  33.1 3.3 %fusion.2 = f32[8,128,128,8]{2,1,3,0:T(8,128)S(1)} fusion(bf16[128,8,8,128]{3,2,1,0:T(8,128)(2,1)} %bitcast.71, bf16[128,8,128,1]{2,1,0,3:T(8,128)(2,1)S(1)} %bitcast.79), kind=kOutput, calls=%fused_computation.7 | convolution fusion | flops 268435456 | bytes 6553600 | tf_op jit(solution)/shard_map/tgsd,ugd->gstu/dot_general | solution.py:136
  36.3 1.1 fusion.36
  37.4 0.0 copy-start.7
  37.4 0.6 divide_convert_fusion
  38.0 1.0 copy-done.7
  39.1 0.7 fusion.16
  39.8 0.5 fusion.12
  40.3 0.0 copy-start.4
  40.3 2.5 %fusion.17 = f32[64,128,64]{1,2,0:T(8,128)} fusion(bf16[64,64,64]{2,1,0:T(8,128)(2,1)S(1)} %copy-done, bf16[128,64,64]{0,1,2:T(8,128)(2,1)S(1)} %fusion.12), kind=kOutput, calls=%fused_computation.22 | convolution fusion | flops 67108864 | bytes 3670016 | tf_op jit(solution)/shard_map/tbj,bkj->tbk/dot_general | solution.py:173
  42.8 2.5 %broadcast_in_dim.17 = f32[128,128,64]{0,2,1:T(8,128)} broadcast(f32[]{:T(128)} %constant.12.clone.1), dimensions={} | broadcast | bytes 4194308 | tf_op jit(solution)/shard_map/broadcast_in_dim | solution.py:175
  45.3 10.5 %scatter_fusion.1 = f32[128,128,64]{0,2,1:T(8,128)} fusion(f32[128,128,64]{0,2,1:T(8,128)} %broadcast_in_dim.17, s32[64]{0:T(128)S(1)} %get-tuple-element.30, f32[64,128,64]{1,2,0:T(8,128)} %fusion.17), kind=kCustom, calls=%fused_computation.1 | custom fusion | flops 524288 | bytes 6291712 | tf_op jit(solution)/shard_map/scatter-add | solution.py:177
  55.8 2.7 %convolution_multiply_fusion = f32[64,64,64]{2,1,0:T(8,128)} fusion(bf16[128,64,64]{0,1,2:T(8,128)(2,1)S(1)} %copy-done.5, bf16[128,64,64]{0,1,2:T(8,128)(2,1)S(1)} %fusion.13), kind=kOutput, calls=%fused_computation.15 | convolution fusion | flops 67371008 | bytes 3145728 | tf_op jit(solution)/shard_map/tbk,tbj->bkj/dot_general | solution.py:162
  58.6 14.5 %all-gather.6.cloned.1.call-done = bf16[1024,1024]{1,0:T(8,128)(2,1)} async-done(((bf16[64,1024]{1,0:T(8,128)(2,1)}), bf16[1024,1024]{1,0:T(8,128)(2,1)}) %all-gather.6.cloned.1.call-update) | async-done | bytes 2097168 | tf_op jit(solution)/shard_map/all_gather | solution.py:39
  73.0 0.0 all-gather.4.cloned.1.call-update
  73.1 2.8 %all_to_all.21 = f32[16,1,16384]{2,1,0:T(1,128)S(1)} reshape(f32[64,64,64]{2,1,0:T(8,128)} %convolution_multiply_fusion) | data formatting | bytes 2097152 | tf_op jit(solution)/shard_map/all_to_all | solution.py:104
  75.9 33.2 %all_to_all.25 = f32[16,1,16384]{2,1,0:T(1,128)S(1)} all-to-all(f32[16,1,16384]{2,1,0:T(1,128)S(1)} %all_to_all.21), channel_id=1, replica_groups=mesh['zl'=2,'x'=4,'c'=2,'zh'=4,'y'=4] {'zh','y'}, dimensions={0} | all-to-all | bytes 2097152 | tf_op jit(solution)/shard_map/all_to_all | solution.py:104
  109.1 0.7 reduce_sum.28
  109.8 12.1 %all_to_all.26 = f32[16,1,1024]{2,1,0:T(1,128)S(1)} all-to-all(f32[16,1,1024]{2,1,0:T(1,128)S(1)} %bitcast.81), channel_id=1, replica_groups=mesh['zl'=2,'x'=4,'c'=2,'zh'=4,'y'=4] {'zl','x','c'}, dimensions={0} | all-to-all | bytes 131072 | tf_op jit(solution)/shard_map/all_to_all | solution.py:106
  121.9 0.1 reduce_sum.29
  121.9 0.7 broadcast_in_dim.32
  122.6 3.7 %all-to-all-start.2 = ((f32[16,1,1024]{2,1,0:T(1,128)}), f32[16,1,1024]{2,1,0:T(1,128)S(1)}, u32[]{:S(2)}, u32[]{:S(2)}) async-start(f32[16,1,1024]{2,1,0:T(1,128)} %broadcast_in_dim.32), calls=%async_computation.2 | async-start | bytes 131072 | tf_op jit(solution)/shard_map/all_to_all | solution.py:108
  126.3 0.9 copy.113.vg_ref
  127.2 1.0 copy.98.sp_ref
  128.2 5.7 %copy.97.sb_ref = f32[128,8192]{1,0:T(8,128)} copy(f32[128,8192]{0,1:T(8,128)} %bitcast.69) | data formatting | bytes 8388608 | tf_op jit(solution)/shard_map/optimization_barrier | solution.py:180
  133.9 0.0 all-to-all-done.2
  133.9 0.2 reduce.2
  134.0 0.7 reshape.66
  134.8 28.4 %all-gather.4.cloned.1.call-done = bf16[16,512,1024]{2,1,0:T(8,128)(2,1)} async-done(((bf16[16,64,1024]{2,1,0:T(8,128)(2,1)}), bf16[16,512,1024]{2,1,0:T(8,128)(2,1)}) %all-gather.4.cloned.1.call-update) | async-done | bytes 16777232 | tf_op jit(solution)/shard_map/all_gather | solution.py:43
  163.2 15.3 %shard_map.103 = (bf16[128,1024]{1,0:T(8,128)(2,1)}, bf16[128,8192]{1,0:T(8,128)(2,1)}) custom-call(bf16[128,8192]{1,0:T(8,128)(2,1)} %tok_ref.1, bf16[8192,1024]{1,0:T(8,128)(2,1)} %bitcast.70, bf16[128,1024]{1,0:T(8,128)(2,1)} %copy.113.vg_ref, f32[128,8192]{1,0:T(8,128)} %copy.97.sb_ref, f32[128,1024]{1,0:T(8,128)} %copy.98.sp_ref), custom_call_target="tpu_custom_call" | custom-call | flops 4294967296 | bytes 26476544 | tf_op jit(solution)/shard_map/pallas_call | solution.py:71
  178.4 1.1 copy.114
  179.6 2.0 %convolution_convert_fusion = bf16[8,128,8,128]{3,1,2,0:T(8,128)(2,1)} fusion(bf16[128,8,128,1]{0,2,3,1:T(8,128)(2,1)S(1)} %bitcast.80, bf16[8,8,128,128]{2,3,1,0:T(8,128)(2,1)S(1)} %copy-done.3), kind=kOutput, calls=%fused_computation.14 | convolution fusion | flops 269484032 | bytes 4456448 | tf_op jit(solution)/shard_map/gstu,ugd->tgsd/dot_general | solution.py:188
  181.6 4.2 %copy.103 = bf16[128,8192]{1,0:T(8,128)(2,1)} copy(bf16[128,8192]{0,1:T(8,128)(2,1)} %bitcast.74) | data formatting | bytes 4194304
  (15 shorter events, 0.1 us)
Async XLA Ops:
  7.2 16.1 %copy-start = (bf16[64,64,64]{2,1,0:T(8,128)(2,1)S(1)}, bf16[64,64,64]{2,1,0:T(8,128)(2,1)}, u32[]{:S(2)}) copy-start(bf16[64,64,64]{2,1,0:T(8,128)(2,1)} %param.13) | copy-start | bytes 1572868
  7.2 65.8 %all-gather.6.cloned.1.call-start = ((), (), s32[]{:S(2)}) async-start(), calls=%async_computation.4 | async-start | bytes 2228224 | tf_op jit(solution)/shard_map/all_gather | solution.py:39
  8.9 154.3 %all-gather.4.cloned.1.call-start = ((), (), s32[]{:S(2)}) async-start(), calls=%async_computation.3 | async-start | bytes 18874368 | tf_op jit(solution)/shard_map/all_gather | solution.py:43
  13.5 4.2 %copy-start.6 = (bf16[128,8192]{1,0:T(8,128)(2,1)S(1)}, bf16[128,8192]{1,0:T(8,128)(2,1)}, u32[]{:S(2)}) copy-start(bf16[128,8192]{1,0:T(8,128)(2,1)} %tok_ref.1) | copy-start | bytes 6291460
  17.7 2.5 %copy-start.9 = (s32[64,2]{0,1:T(2,128)S(1)}, s32[64,2]{0,1:T(2,128)}, u32[]{:S(2)}) copy-start(s32[64,2]{0,1:T(2,128)} %param.14) | copy-start | bytes 1540
  25.9 7.1 %copy-start.8 = (s32[1,128]{1,0:T(1,128)S(1)}, s32[1,128]{1,0:T(1,128)}, u32[]{:S(2)}) copy-start(s32[1,128]{1,0:T(1,128)} %param.11) | copy-start | bytes 1540
  37.4 1.7 copy-start.7
  38.0 1.8 copy-start.2
  40.3 2.5 %copy-start.4 = (bf16[128,64,64]{0,1,2:T(8,128)(2,1)}, bf16[128,64,64]{0,1,2:T(8,128)(2,1)S(1)}, u32[]{:S(2)}) copy-start(bf16[128,64,64]{0,1,2:T(8,128)(2,1)S(1)} %fusion.12) | copy-start | bytes 3145732
  45.3 10.5 %copy-start.5 = (bf16[128,64,64]{0,1,2:T(8,128)(2,1)S(1)}, bf16[128,64,64]{0,1,2:T(8,128)(2,1)}, u32[]{:S(2)}) copy-start(bf16[128,64,64]{0,1,2:T(8,128)(2,1)} %copy-done.4) | copy-start | bytes 3145732
  122.6 11.3 %all-to-all-start.2 = ((f32[16,1,1024]{2,1,0:T(1,128)}), f32[16,1,1024]{2,1,0:T(1,128)S(1)}, u32[]{:S(2)}, u32[]{:S(2)}) async-start(f32[16,1,1024]{2,1,0:T(1,128)} %broadcast_in_dim.32), calls=%async_computation.2 | async-start | bytes 131072 | tf_op jit(solution)/shard_map/all_to_all | solution.py:108
  163.2 16.4 %copy-start.3 = (bf16[8,8,128,128]{2,3,1,0:T(8,128)(2,1)S(1)}, bf16[8,8,128,128]{2,3,1,0:T(8,128)(2,1)}, u32[]{:S(2)}) copy-start(bf16[8,8,128,128]{2,3,1,0:T(8,128)(2,1)} %copy-done.2) | copy-start | bytes 6291460
  181.6 4.2 %copy-start.1 = (bf16[64,64,64]{2,1,0:T(8,128)(2,1)S(1)}, bf16[64,64,64]{2,1,0:T(8,128)(2,1)}, u32[]{:S(2)}) copy-start(bf16[64,64,64]{2,1,0:T(8,128)(2,1)} %param.13) | copy-start | bytes 1572868
Sparse Core Ops, SparseCore 0:
  11.0 61.9 all-gather.5
  74.9 88.2 all-gather.3

commit v7 on v6

--- a/solution.py
+++ b/solution.py
@@ -66,7 +66,7 @@
 def dense_tail(tokens, full_weight, value_grad, spread_back, sparse_part):
     rows, depth = tokens.shape
     width = full_weight.shape[1]
-    tile = 1024
+    tile = 2048
     steps = depth // tile
     return pl.pallas_call(
         tail_kernel,

time: 194 us -> 193 us (level)
  no operation moved by 1% of the time
where the time goes in v7:
time: 193 us; the launch traced here: 192 us
  blocking collectives  45.7 us (24%)
  waiting for transfers between devices  42.4 us (22%)
  local copies, waits for them, and re-layouts  33.5 us (17%)
  other arithmetic  20.3 us (11%)
  matrix products  17.4 us (9%)
  Pallas kernels  14.2 us (7%)
  between operations  14.2 us (7%)
  starting transfers between devices  3.81 us (2%)
    all_to_all x1, blocking collectives, reduce_delta(): mine = lax.all_to_all(flat, SHARD, 0, 0, tiled=False).sum(0)  33.1 us
    all_gather x1, waiting for transfers between devices, gather_rest(): whole = lax.all_gather(by_shard, PIECE, axis=1, tiled=True)  28.2 us
    pallas_call x1, Pallas kernels, dense_tail(): pl.pallas_call(tail_kernel, grid=(steps,), in_specs=[pl.BlockSpec((rows,...  14.2 us
    all_gather x1, waiting for transfers between devices, gather_pieces(): return lax.all_gather(piece, SHARD, axis=0, tiled=False)  14.2 us
    all_to_all x1, blocking collectives, reduce_delta(): part = lax.all_to_all(mine, REPLICA, 0, 0, tiled=False).sum(0)  12.6 us
    unnamed x24, local copies, waits for them, and re-layouts  12.2 us
    scatter-add x1, other arithmetic, local(): spread_back = jnp.zeros((tok_rows, D // BLK, BLK), jnp.float32).at[:, row...  10.6 us
    scatter-add x1, other arithmetic, local(): sparse_part = jnp.zeros((tok_rows, KVH * HD // BLK, BLK), jnp.float32).at...  7.04 us
  transfers between devices with their start and end apart: 3, of which 2 were waited for; matrix products, arithmetic and copies ran while one was open for 30% of the time, Pallas kernels for 0%

profile of v7, /device:TPU:1, one launch (start us, length us, event | category | flops | bytes accessed | tf_op | source)
XLA Modules:
  0.0 191.6 jit_solution(4188395710244508986)
XLA Ops:
  7.2 0.0 copy-start
  7.2 0.0 all-gather.6.cloned.1.call-start
  7.2 1.6 constant_dynamic-slice_fusion
  8.9 0.0 all-gather.6.cloned.1.call-update
  8.9 0.0 all-gather.4.cloned.1.call-start
  9.0 1.0 copy.116
  10.0 3.5 %copy.117 = bf16[16,8,64,128]{3,2,1,0:T(8,128)(2,1)} copy(bf16[16,8,64,128]{3,1,2,0:T(8,128)(2,1)} %bitcast.77) | data formatting | bytes 4194304
  13.5 4.2 %copy.112 = bf16[128,8192]{0,1:T(8,128)(2,1)} copy(bf16[128,8192]{1,0:T(8,128)(2,1)} %param.15) | data formatting | bytes 4194304 | tf_op jit(solution)/shard_map/reshape | solution.py:146
  17.7 2.5 %copy.84 = bf16[128,8192]{0,1:T(8,128)(2,1)} copy(bf16[128,8192]{1,0:T(8,128)(2,1)S(1)} %copy-done.6) | data formatting | bytes 4194304 | tf_op args[0]
  20.1 0.0 copy-done.9
  20.2 3.1 %fusion.13 = bf16[128,64,64]{0,1,2:T(8,128)(2,1)S(1)} fusion(bf16[128,128,64]{0,2,1:T(8,128)(2,1)} %bitcast.73, s32[64]{0:T(128)S(1)} %get-tuple-element.33), kind=kOutput, calls=%fused_computation.19 | convolution fusion | flops 134750208 | bytes 3145984 | tf_op jit(solution)/shard_map/trk,br->tbk/dot_general | solution.py:128
  23.2 0.0 copy-done
  23.3 2.6 %fusion.20 = f32[64,128,64]{1,2,0:T(8,128)} fusion(bf16[64,64,64]{2,1,0:T(8,128)(2,1)S(1)} %copy-done, bf16[128,64,64]{0,1,2:T(8,128)(2,1)S(1)} %fusion.13), kind=kOutput, calls=%fused_computation.25 | convolution fusion | flops 67108864 | bytes 3670016 | tf_op jit(solution)/shard_map/tbk,bkj->tbj/dot_general | solution.py:164
  25.9 0.0 copy-start.8
  25.9 7.0 %scatter_fusion = f32[128,16,64]{0,2,1:T(8,128)S(1)} fusion(f32[128,16,64]{0,2,1:T(8,128)S(1)} %broadcast_in_dim.16, s32[64]{0:T(128)S(1)} %get-tuple-element.31, f32[64,128,64]{1,2,0:T(8,128)} %fusion.20), kind=kCustom, calls=%fused_computation | custom fusion | flops 524288 | bytes 6291712 | tf_op jit(solution)/shard_map/scatter-add | solution.py:170
  33.0 0.1 fusion.25
  33.1 3.3 %fusion.2 = f32[8,128,128,8]{2,1,3,0:T(8,128)S(1)} fusion(bf16[128,8,8,128]{3,2,1,0:T(8,128)(2,1)} %bitcast.71, bf16[128,8,128,1]{2,1,0,3:T(8,128)(2,1)S(1)} %bitcast.79), kind=kOutput, calls=%fused_computation.7 | convolution fusion | flops 268435456 | bytes 6553600 | tf_op jit(solution)/shard_map/tgsd,ugd->gstu/dot_general | solution.py:136
  36.3 1.1 fusion.36
  37.4 0.0 copy-start.7
  37.4 0.6 divide_convert_fusion
  38.0 1.0 copy-done.7
  39.1 0.7 fusion.16
  39.8 0.5 fusion.12
  40.3 0.0 copy-start.4
  40.3 2.5 %fusion.17 = f32[64,128,64]{1,2,0:T(8,128)} fusion(bf16[64,64,64]{2,1,0:T(8,128)(2,1)S(1)} %copy-done, bf16[128,64,64]{0,1,2:T(8,128)(2,1)S(1)} %fusion.12), kind=kOutput, calls=%fused_computation.22 | convolution fusion | flops 67108864 | bytes 3670016 | tf_op jit(solution)/shard_map/tbj,bkj->tbk/dot_general | solution.py:173
  42.8 2.5 %broadcast_in_dim.17 = f32[128,128,64]{0,2,1:T(8,128)} broadcast(f32[]{:T(128)} %constant.12.clone.1), dimensions={} | broadcast | bytes 4194308 | tf_op jit(solution)/shard_map/broadcast_in_dim | solution.py:175
  45.3 10.6 %scatter_fusion.1 = f32[128,128,64]{0,2,1:T(8,128)} fusion(f32[128,128,64]{0,2,1:T(8,128)} %broadcast_in_dim.17, s32[64]{0:T(128)S(1)} %get-tuple-element.30, f32[64,128,64]{1,2,0:T(8,128)} %fusion.17), kind=kCustom, calls=%fused_computation.1 | custom fusion | flops 524288 | bytes 6291712 | tf_op jit(solution)/shard_map/scatter-add | solution.py:177
  55.9 2.7 %convolution_multiply_fusion = f32[64,64,64]{2,1,0:T(8,128)} fusion(bf16[128,64,64]{0,1,2:T(8,128)(2,1)S(1)} %copy-done.5, bf16[128,64,64]{0,1,2:T(8,128)(2,1)S(1)} %fusion.13), kind=kOutput, calls=%fused_computation.15 | convolution fusion | flops 67371008 | bytes 3145728 | tf_op jit(solution)/shard_map/tbk,tbj->bkj/dot_general | solution.py:162
  58.6 14.2 %all-gather.6.cloned.1.call-done = bf16[1024,1024]{1,0:T(8,128)(2,1)} async-done(((bf16[64,1024]{1,0:T(8,128)(2,1)}), bf16[1024,1024]{1,0:T(8,128)(2,1)}) %all-gather.6.cloned.1.call-update) | async-done | bytes 2097168 | tf_op jit(solution)/shard_map/all_gather | solution.py:39
  72.8 0.0 all-gather.4.cloned.1.call-update
  72.8 2.8 %all_to_all.21 = f32[16,1,16384]{2,1,0:T(1,128)S(1)} reshape(f32[64,64,64]{2,1,0:T(8,128)} %convolution_multiply_fusion) | data formatting | bytes 2097152 | tf_op jit(solution)/shard_map/all_to_all | solution.py:104
  75.7 33.1 %all_to_all.25 = f32[16,1,16384]{2,1,0:T(1,128)S(1)} all-to-all(f32[16,1,16384]{2,1,0:T(1,128)S(1)} %all_to_all.21), channel_id=1, replica_groups=mesh['zl'=2,'x'=4,'c'=2,'zh'=4,'y'=4] {'zh','y'}, dimensions={0} | all-to-all | bytes 2097152 | tf_op jit(solution)/shard_map/all_to_all | solution.py:104
  108.8 0.7 reduce_sum.28
  109.5 12.6 %all_to_all.26 = f32[16,1,1024]{2,1,0:T(1,128)S(1)} all-to-all(f32[16,1,1024]{2,1,0:T(1,128)S(1)} %bitcast.81), channel_id=1, replica_groups=mesh['zl'=2,'x'=4,'c'=2,'zh'=4,'y'=4] {'zl','x','c'}, dimensions={0} | all-to-all | bytes 131072 | tf_op jit(solution)/shard_map/all_to_all | solution.py:106
  122.1 0.1 reduce_sum.29
  122.1 0.7 broadcast_in_dim.32
  122.8 3.7 %all-to-all-start.2 = ((f32[16,1,1024]{2,1,0:T(1,128)}), f32[16,1,1024]{2,1,0:T(1,128)S(1)}, u32[]{:S(2)}, u32[]{:S(2)}) async-start(f32[16,1,1024]{2,1,0:T(1,128)} %broadcast_in_dim.32), calls=%async_computation.2 | async-start | bytes 131072 | tf_op jit(solution)/shard_map/all_to_all | solution.py:108
  126.5 0.9 copy.113.vg_ref
  127.4 1.0 copy.98.sp_ref
  128.4 5.7 %copy.97.sb_ref = f32[128,8192]{1,0:T(8,128)} copy(f32[128,8192]{0,1:T(8,128)} %bitcast.69) | data formatting | bytes 8388608 | tf_op jit(solution)/shard_map/optimization_barrier | solution.py:180
  134.1 0.0 all-to-all-done.2
  134.1 0.2 reduce.2
  134.2 0.7 reshape.66
  135.0 28.2 %all-gather.4.cloned.1.call-done = bf16[16,512,1024]{2,1,0:T(8,128)(2,1)} async-done(((bf16[16,64,1024]{2,1,0:T(8,128)(2,1)}), bf16[16,512,1024]{2,1,0:T(8,128)(2,1)}) %all-gather.4.cloned.1.call-update) | async-done | bytes 16777232 | tf_op jit(solution)/shard_map/all_gather | solution.py:43
  163.2 14.2 %shard_map.103 = (bf16[128,1024]{1,0:T(8,128)(2,1)}, bf16[128,8192]{1,0:T(8,128)(2,1)}) custom-call(bf16[128,8192]{1,0:T(8,128)(2,1)} %tok_ref.1, bf16[8192,1024]{1,0:T(8,128)(2,1)} %bitcast.70, bf16[128,1024]{1,0:T(8,128)(2,1)} %copy.113.vg_ref, f32[128,8192]{1,0:T(8,128)} %copy.97.sb_ref, f32[128,1024]{1,0:T(8,128)} %copy.98.sp_ref), custom_call_target="tpu_custom_call" | custom-call | flops 4294967296 | bytes 26476544 | tf_op jit(solution)/shard_map/pallas_call | solution.py:71
  177.4 1.1 copy.114
  178.5 2.0 %convolution_convert_fusion = bf16[8,128,8,128]{3,1,2,0:T(8,128)(2,1)} fusion(bf16[128,8,128,1]{0,2,3,1:T(8,128)(2,1)S(1)} %bitcast.80, bf16[8,8,128,128]{2,3,1,0:T(8,128)(2,1)S(1)} %copy-done.3), kind=kOutput, calls=%fused_computation.14 | convolution fusion | flops 269484032 | bytes 4456448 | tf_op jit(solution)/shard_map/gstu,ugd->tgsd/dot_general | solution.py:188
  180.6 4.2 %copy.103 = bf16[128,8192]{1,0:T(8,128)(2,1)} copy(bf16[128,8192]{0,1:T(8,128)(2,1)} %bitcast.74) | data formatting | bytes 4194304
  (15 shorter events, 0.1 us)
Async XLA Ops:
  7.2 16.1 %copy-start = (bf16[64,64,64]{2,1,0:T(8,128)(2,1)S(1)}, bf16[64,64,64]{2,1,0:T(8,128)(2,1)}, u32[]{:S(2)}) copy-start(bf16[64,64,64]{2,1,0:T(8,128)(2,1)} %param.13) | copy-start | bytes 1572868
  7.2 65.6 %all-gather.6.cloned.1.call-start = ((), (), s32[]{:S(2)}) async-start(), calls=%async_computation.4 | async-start | bytes 2228224 | tf_op jit(solution)/shard_map/all_gather | solution.py:39
  8.9 154.3 %all-gather.4.cloned.1.call-start = ((), (), s32[]{:S(2)}) async-start(), calls=%async_computation.3 | async-start | bytes 18874368 | tf_op jit(solution)/shard_map/all_gather | solution.py:43
  13.5 4.2 %copy-start.6 = (bf16[128,8192]{1,0:T(8,128)(2,1)S(1)}, bf16[128,8192]{1,0:T(8,128)(2,1)}, u32[]{:S(2)}) copy-start(bf16[128,8192]{1,0:T(8,128)(2,1)} %tok_ref.1) | copy-start | bytes 6291460
  17.7 2.5 %copy-start.9 = (s32[64,2]{0,1:T(2,128)S(1)}, s32[64,2]{0,1:T(2,128)}, u32[]{:S(2)}) copy-start(s32[64,2]{0,1:T(2,128)} %param.14) | copy-start | bytes 1540
  25.9 7.1 %copy-start.8 = (s32[1,128]{1,0:T(1,128)S(1)}, s32[1,128]{1,0:T(1,128)}, u32[]{:S(2)}) copy-start(s32[1,128]{1,0:T(1,128)} %param.11) | copy-start | bytes 1540
  37.4 1.7 copy-start.7
  38.0 1.8 copy-start.2
  40.3 2.5 %copy-start.4 = (bf16[128,64,64]{0,1,2:T(8,128)(2,1)}, bf16[128,64,64]{0,1,2:T(8,128)(2,1)S(1)}, u32[]{:S(2)}) copy-start(bf16[128,64,64]{0,1,2:T(8,128)(2,1)S(1)} %fusion.12) | copy-start | bytes 3145732
  45.3 10.6 %copy-start.5 = (bf16[128,64,64]{0,1,2:T(8,128)(2,1)S(1)}, bf16[128,64,64]{0,1,2:T(8,128)(2,1)}, u32[]{:S(2)}) copy-start(bf16[128,64,64]{0,1,2:T(8,128)(2,1)} %copy-done.4) | copy-start | bytes 3145732
  122.8 11.3 %all-to-all-start.2 = ((f32[16,1,1024]{2,1,0:T(1,128)}), f32[16,1,1024]{2,1,0:T(1,128)S(1)}, u32[]{:S(2)}, u32[]{:S(2)}) async-start(f32[16,1,1024]{2,1,0:T(1,128)} %broadcast_in_dim.32), calls=%async_computation.2 | async-start | bytes 131072 | tf_op jit(solution)/shard_map/all_to_all | solution.py:108
  163.2 15.4 %copy-start.3 = (bf16[8,8,128,128]{2,3,1,0:T(8,128)(2,1)S(1)}, bf16[8,8,128,128]{2,3,1,0:T(8,128)(2,1)}, u32[]{:S(2)}) copy-start(bf16[8,8,128,128]{2,3,1,0:T(8,128)(2,1)} %copy-done.2) | copy-start | bytes 6291460
  180.6 4.2 %copy-start.1 = (bf16[64,64,64]{2,1,0:T(8,128)(2,1)S(1)}, bf16[64,64,64]{2,1,0:T(8,128)(2,1)}, u32[]{:S(2)}) copy-start(bf16[64,64,64]{2,1,0:T(8,128)(2,1)} %param.13) | copy-start | bytes 1572868
Sparse Core Ops, SparseCore 0:
  11.0 61.7 all-gather.5
  74.6 88.4 all-gather.3

commit v8 on v7

--- a/solution.py
+++ b/solution.py
@@ -44,7 +44,7 @@
     return whole.reshape(-1, whole.shape[-1])
 
 
-def tail_kernel(tok_ref, w_ref, vg_ref, sb_ref, sp_ref, val_ref, ig_ref, acc_ref):
+def tail_kernel(tok_ref, w_ref, vg_ref, sb_ref, sp_ref, pr_ref, att_ref, ig_ref, acc_ref):
     k = pl.program_id(0)
 
     @pl.when(k == 0)
@@ -60,10 +60,18 @@
 
     @pl.when(k == pl.num_programs(0) - 1)
     def _():
-        val_ref[...] = acc_ref[...].astype(val_ref.dtype)
-
-
-def dense_tail(tokens, full_weight, value_grad, spread_back, sparse_part):
+        values = acc_ref[...].astype(jnp.bfloat16)
+        kv_heads, groups = pr_ref.shape[0], pr_ref.shape[1]
+        for g in range(kv_heads):
+            head = values[:, g * HD : (g + 1) * HD]
+            for q in range(groups):
+                col = (g * groups + q) * HD
+                att_ref[:, col : col + HD] = jnp.dot(
+                    pr_ref[g, q], head, preferred_element_type=jnp.float32
+                ).astype(att_ref.dtype)
+
+
+def dense_tail(tokens, full_weight, value_grad, spread_back, sparse_part, attn_probs):
     rows, depth = tokens.shape
     width = full_weight.shape[1]
     tile = 2048
@@ -77,13 +85,14 @@
             pl.BlockSpec((rows, width), lambda k: (0, 0)),
             pl.BlockSpec((rows, tile), lambda k: (0, k)),
             pl.BlockSpec((rows, width), lambda k: (0, 0)),
+            pl.BlockSpec(attn_probs.shape, lambda k: (0, 0, 0, 0)),
         ],
         out_specs=[
-            pl.BlockSpec((rows, width), lambda k: (0, 0)),
+            pl.BlockSpec((rows, QH * HD), lambda k: (0, 0)),
             pl.BlockSpec((rows, tile), lambda k: (0, k)),
         ],
         out_shape=[
-            jax.ShapeDtypeStruct((rows, width), jnp.bfloat16),
+            jax.ShapeDtypeStruct((rows, QH * HD), jnp.bfloat16),
             jax.ShapeDtypeStruct((rows, depth), jnp.bfloat16),
         ],
         scratch_shapes=[pltpu.VMEM((rows, width), jnp.float32)],
@@ -93,7 +102,7 @@
             bytes_accessed=2 * depth * width + 8 * rows * depth + 10 * rows * width,
             transcendentals=0,
         ),
-    )(tokens, full_weight, value_grad, spread_back, sparse_part)
+    )(tokens, full_weight, value_grad, spread_back, sparse_part, attn_probs)
 
 
 def reduce_delta(grad_term):
@@ -182,12 +191,8 @@
     )
     full_weight = gather_rest(by_shard)
     delta_grad = reduce_delta(grad_term)
-    values, input_grad = dense_tail(tokens, full_weight, value_grad, spread_back, sparse_part)
-    value_heads = values.reshape(tok_rows, KVH, HD)
-    attention = (
-        jnp.einsum("gstu,ugd->tgsd", attn_probs, value_heads, preferred_element_type=jnp.float32)
-        .reshape(tok_rows, QH * HD)
-        .astype(jnp.bfloat16)
+    attention, input_grad = dense_tail(
+        tokens, full_weight, value_grad, spread_back, sparse_part, attn_probs
     )
     return (attention, input_grad, delta_grad)
 

time: 193 us -> 187 us (0.969)
  local copies, waits for them, and re-layouts: 33.5 us -> 27.6 us
  waiting for transfers between devices: 42.4 us -> 40.2 us
  other arithmetic: 20.3 us -> 22.4 us
  Pallas kernels: 14.2 us -> 16.2 us
    unnamed x24 -> x21, local copies, waits for them, and re-layouts: 12.2 us -> 7.59 us
    all_gather x1, waiting for transfers between devices: 14.2 us -> 11.7 us  [gather_pieces(): return lax.all_gather(piece, SHARD, axis=0, tiled=False)]
    dot_general x1 -> x0, matrix products: 2.04 us -> none  [local(): jnp.einsum('gstu,ugd->tgsd', attn_probs, value_heads, preferred_element_t...]
  transfers between devices with their start and end apart: 3 -> 3, of which waited for: 2 -> 2; matrix products, arithmetic and copies ran while one was open for 30% -> 33% of each run, Pallas kernels for 0% -> 0%
where the time goes in v8:
time: 187 us; the launch traced here: 186 us
  blocking collectives  45.6 us (24%)
  waiting for transfers between devices  40.2 us (21%)
  local copies, waits for them, and re-layouts  27.6 us (15%)
  other arithmetic  22.4 us (12%)
  Pallas kernels  16.2 us (9%)
  matrix products  16.1 us (9%)
  between operations  14.2 us (8%)
  starting transfers between devices  3.82 us (2%)
    all_to_all x1, blocking collectives, reduce_delta(): mine = lax.all_to_all(flat, SHARD, 0, 0, tiled=False).sum(0)  33.2 us
    all_gather x1, waiting for transfers between devices, gather_rest(): whole = lax.all_gather(by_shard, PIECE, axis=1, tiled=True)  28.5 us
    pallas_call x1, Pallas kernels, dense_tail(): pl.pallas_call(tail_kernel, grid=(steps,), in_specs=[pl.BlockSpec((rows,...  16.2 us
    all_to_all x1, blocking collectives, reduce_delta(): part = lax.all_to_all(mine, REPLICA, 0, 0, tiled=False).sum(0)  12.4 us
    all_gather x1, waiting for transfers between devices, gather_pieces(): return lax.all_gather(piece, SHARD, axis=0, tiled=False)  11.7 us
    scatter-add x1, other arithmetic, local(): spread_back = jnp.zeros((tok_rows, D // BLK, BLK), jnp.float32).at[:, row...  10.7 us
    unnamed x21, local copies, waits for them, and re-layouts  7.59 us
    scatter-add x1, other arithmetic, local(): sparse_part = jnp.zeros((tok_rows, KVH * HD // BLK, BLK), jnp.float32).at...  7.04 us
  transfers between devices with their start and end apart: 3, of which 2 were waited for; matrix products, arithmetic and copies ran while one was open for 33% of the time, Pallas kernels for 0%

profile of v8, /device:TPU:1, one launch (start us, length us, event | category | flops | bytes accessed | tf_op | source)
XLA Modules:
  0.0 186.2 jit_solution(13486930302696200644)
XLA Ops:
  7.2 0.0 copy-start
  7.2 0.0 all-gather.6.cloned.1.call-start
  7.2 1.6 constant_dynamic-slice_fusion
  8.9 0.0 all-gather.6.cloned.1.call-update
  8.9 0.0 all-gather.4.cloned.1.call-start
  9.0 1.0 copy.98
  10.0 3.5 %copy.99 = bf16[16,8,64,128]{3,2,1,0:T(8,128)(2,1)} copy(bf16[16,8,64,128]{3,1,2,0:T(8,128)(2,1)} %bitcast.66) | data formatting | bytes 4194304
  13.5 4.2 %copy.95 = bf16[128,8192]{0,1:T(8,128)(2,1)} copy(bf16[128,8192]{1,0:T(8,128)(2,1)} %param.15) | data formatting | bytes 4194304 | tf_op jit(solution)/shard_map/reshape | solution.py:155
  17.7 0.0 copy-done.5
  17.7 2.5 %copy.72 = bf16[128,8192]{0,1:T(8,128)(2,1)} copy(bf16[128,8192]{1,0:T(8,128)(2,1)S(1)} %copy-done.5) | data formatting | bytes 4194304 | tf_op args[0]
  20.1 0.0 copy-done.8
  20.2 3.1 %fusion.13 = bf16[128,64,64]{0,1,2:T(8,128)(2,1)S(1)} fusion(bf16[128,128,64]{0,2,1:T(8,128)(2,1)} %bitcast.63, s32[64]{0:T(128)S(1)} %get-tuple-element.18), kind=kOutput, calls=%fused_computation.18 | convolution fusion | flops 134750208 | bytes 3145984 | tf_op jit(solution)/shard_map/trk,br->tbk/dot_general | solution.py:137
  23.2 0.0 copy-done
  23.3 2.6 %fusion.20 = f32[64,128,64]{1,2,0:T(8,128)} fusion(bf16[64,64,64]{2,1,0:T(8,128)(2,1)S(1)} %copy-done, bf16[128,64,64]{0,1,2:T(8,128)(2,1)S(1)} %fusion.13), kind=kOutput, calls=%fused_computation.24 | convolution fusion | flops 67108864 | bytes 3670016 | tf_op jit(solution)/shard_map/tbk,bkj->tbj/dot_general | solution.py:173
  25.9 0.0 copy-start.7
  25.9 7.0 %scatter_fusion = f32[128,16,64]{0,2,1:T(8,128)S(1)} fusion(f32[128,16,64]{0,2,1:T(8,128)S(1)} %broadcast_in_dim.16, s32[64]{0:T(128)S(1)} %get-tuple-element.16, f32[64,128,64]{1,2,0:T(8,128)} %fusion.20), kind=kCustom, calls=%fused_computation | custom fusion | flops 524288 | bytes 6291712 | tf_op jit(solution)/shard_map/scatter-add | solution.py:179
  33.0 0.0 copy-done.7
  33.0 0.1 fusion.25
  33.1 4.1 %fusion.2 = f32[8,128,128,8]{1,2,3,0:T(8,128)S(1)} fusion(bf16[128,8,8,128]{3,2,1,0:T(8,128)(2,1)} %bitcast.61, bf16[128,8,128,1]{2,1,0,3:T(8,128)(2,1)S(1)} %bitcast.68), kind=kOutput, calls=%fused_computation.7 | convolution fusion | flops 268435456 | bytes 6553600 | tf_op jit(solution)/shard_map/tgsd,ugd->gstu/dot_general | solution.py:145
  37.1 2.4 %fusion.36 = (f32[8,8,128]{2,1,0:T(8,128)S(1)}, f32[8,8,128,128]{3,2,1,0:T(8,128)S(1)}) fusion(f32[8,128,128,8]{1,2,3,0:T(8,128)S(1)} %fusion.2, pred[128,128]{1,0:T(8,128)(4,1)S(1)} %fusion.25), kind=kOutput, calls=%fused_computation.46 | output fusion | flops 6291583 | bytes 8437760 | tf_op jit(solution)/shard_map/sub | solution.py:153
  39.6 0.0 copy-start.6
  39.6 1.3 divide_convert_fusion.pr_ref
  40.8 0.3 copy-done.6
  41.1 0.7 fusion.16
  41.8 0.3 copy-done.2
  42.1 0.5 fusion.12
  42.6 0.0 copy-start.3
  42.6 2.5 %fusion.17 = f32[64,128,64]{1,2,0:T(8,128)} fusion(bf16[64,64,64]{2,1,0:T(8,128)(2,1)S(1)} %copy-done, bf16[128,64,64]{0,1,2:T(8,128)(2,1)S(1)} %fusion.12), kind=kOutput, calls=%fused_computation.21 | convolution fusion | flops 67108864 | bytes 3670016 | tf_op jit(solution)/shard_map/tbj,bkj->tbk/dot_general | solution.py:182
  45.1 2.5 %broadcast_in_dim.17 = f32[128,128,64]{0,2,1:T(8,128)} broadcast(f32[]{:T(128)} %constant.12.clone.1), dimensions={} | broadcast | bytes 4194308 | tf_op jit(solution)/shard_map/broadcast_in_dim | solution.py:184
  47.6 10.7 %scatter_fusion.1 = f32[128,128,64]{0,2,1:T(8,128)} fusion(f32[128,128,64]{0,2,1:T(8,128)} %broadcast_in_dim.17, s32[64]{0:T(128)S(1)} %get-tuple-element.15, f32[64,128,64]{1,2,0:T(8,128)} %fusion.17), kind=kCustom, calls=%fused_computation.1 | custom fusion | flops 524288 | bytes 6291712 | tf_op jit(solution)/shard_map/scatter-add | solution.py:186
  58.3 2.7 %convolution_multiply_fusion = f32[64,64,64]{2,1,0:T(8,128)} fusion(bf16[128,64,64]{0,1,2:T(8,128)(2,1)S(1)} %copy-done.4, bf16[128,64,64]{0,1,2:T(8,128)(2,1)S(1)} %fusion.13), kind=kOutput, calls=%fused_computation.14 | convolution fusion | flops 67371008 | bytes 3145728 | tf_op jit(solution)/shard_map/tbk,tbj->bkj/dot_general | solution.py:171
  61.1 11.7 %all-gather.6.cloned.1.call-done = bf16[1024,1024]{1,0:T(8,128)(2,1)} async-done(((bf16[64,1024]{1,0:T(8,128)(2,1)}), bf16[1024,1024]{1,0:T(8,128)(2,1)}) %all-gather.6.cloned.1.call-update) | async-done | bytes 2097168 | tf_op jit(solution)/shard_map/all_gather | solution.py:39
  72.8 0.0 all-gather.4.cloned.1.call-update
  72.8 2.7 %all_to_all.21 = f32[16,1,16384]{2,1,0:T(1,128)S(1)} reshape(f32[64,64,64]{2,1,0:T(8,128)} %convolution_multiply_fusion) | data formatting | bytes 2097152 | tf_op jit(solution)/shard_map/all_to_all | solution.py:113
  75.4 33.2 %all_to_all.25 = f32[16,1,16384]{2,1,0:T(1,128)S(1)} all-to-all(f32[16,1,16384]{2,1,0:T(1,128)S(1)} %all_to_all.21), channel_id=1, replica_groups=mesh['zl'=2,'x'=4,'c'=2,'zh'=4,'y'=4] {'zh','y'}, dimensions={0} | all-to-all | bytes 2097152 | tf_op jit(solution)/shard_map/all_to_all | solution.py:113
  108.6 0.7 reduce_sum.28
  109.3 12.4 %all_to_all.26 = f32[16,1,1024]{2,1,0:T(1,128)S(1)} all-to-all(f32[16,1,1024]{2,1,0:T(1,128)S(1)} %bitcast.69), channel_id=1, replica_groups=mesh['zl'=2,'x'=4,'c'=2,'zh'=4,'y'=4] {'zl','x','c'}, dimensions={0} | all-to-all | bytes 131072 | tf_op jit(solution)/shard_map/all_to_all | solution.py:115
  121.7 0.1 reduce_sum.29
  121.8 0.7 broadcast_in_dim.32
  122.5 3.7 %all-to-all-start.2 = ((f32[16,1,1024]{2,1,0:T(1,128)}), f32[16,1,1024]{2,1,0:T(1,128)S(1)}, u32[]{:S(2)}, u32[]{:S(2)}) async-start(f32[16,1,1024]{2,1,0:T(1,128)} %broadcast_in_dim.32), calls=%async_computation.2 | async-start | bytes 131072 | tf_op jit(solution)/shard_map/all_to_all | solution.py:117
  126.2 0.9 copy.96.vg_ref
  127.1 1.0 copy.86.sp_ref
  128.1 5.7 %copy.85.sb_ref = f32[128,8192]{1,0:T(8,128)} copy(f32[128,8192]{0,1:T(8,128)} %bitcast.59) | data formatting | bytes 8388608 | tf_op jit(solution)/shard_map/optimization_barrier | solution.py:189
  133.8 0.0 all-to-all-done.2
  133.8 0.2 reduce.2
  133.9 0.7 reshape.60
  134.7 28.5 %all-gather.4.cloned.1.call-done = bf16[16,512,1024]{2,1,0:T(8,128)(2,1)} async-done(((bf16[16,64,1024]{2,1,0:T(8,128)(2,1)}), bf16[16,512,1024]{2,1,0:T(8,128)(2,1)}) %all-gather.4.cloned.1.call-update) | async-done | bytes 16777232 | tf_op jit(solution)/shard_map/all_gather | solution.py:43
  163.2 16.2 %shard_map.103 = (bf16[128,8192]{1,0:T(8,128)(2,1)}, bf16[128,8192]{1,0:T(8,128)(2,1)}) custom-call(bf16[128,8192]{1,0:T(8,128)(2,1)} %tok_ref.1, bf16[8192,1024]{1,0:T(8,128)(2,1)} %bitcast.60, bf16[128,1024]{1,0:T(8,128)(2,1)} %copy.96.vg_ref, f32[128,8192]{1,0:T(8,128)} %copy.85.sb_ref, f32[128,1024]{1,0:T(8,128)} %copy.86.sp_ref, ...), custom_call_target="tpu_custom_call" | custom-call | flops 4294967296 | bytes 26476544 | tf_op jit(solution)/shard_map/pallas_call | solution.py:79
  (10 shorter events, 0.1 us)
Async XLA Ops:
  7.2 16.1 %copy-start = (bf16[64,64,64]{2,1,0:T(8,128)(2,1)S(1)}, bf16[64,64,64]{2,1,0:T(8,128)(2,1)}, u32[]{:S(2)}) copy-start(bf16[64,64,64]{2,1,0:T(8,128)(2,1)} %param.13) | copy-start | bytes 1572868
  7.2 65.6 %all-gather.6.cloned.1.call-start = ((), (), s32[]{:S(2)}) async-start(), calls=%async_computation.4 | async-start | bytes 2228224 | tf_op jit(solution)/shard_map/all_gather | solution.py:39
  8.9 154.3 %all-gather.4.cloned.1.call-start = ((), (), s32[]{:S(2)}) async-start(), calls=%async_computation.3 | async-start | bytes 18874368 | tf_op jit(solution)/shard_map/all_gather | solution.py:43
  13.5 4.2 %copy-start.5 = (bf16[128,8192]{1,0:T(8,128)(2,1)S(1)}, bf16[128,8192]{1,0:T(8,128)(2,1)}, u32[]{:S(2)}) copy-start(bf16[128,8192]{1,0:T(8,128)(2,1)} %tok_ref.1) | copy-start | bytes 6291460
  17.7 2.5 %copy-start.8 = (s32[64,2]{0,1:T(2,128)S(1)}, s32[64,2]{0,1:T(2,128)}, u32[]{:S(2)}) copy-start(s32[64,2]{0,1:T(2,128)} %param.14) | copy-start | bytes 1540
  25.9 7.1 %copy-start.7 = (s32[1,128]{1,0:T(1,128)S(1)}, s32[1,128]{1,0:T(1,128)}, u32[]{:S(2)}) copy-start(s32[1,128]{1,0:T(1,128)} %param.11) | copy-start | bytes 1540
  39.6 1.6 copy-start.6
  40.8 1.3 copy-start.2
  42.6 2.5 %copy-start.3 = (bf16[128,64,64]{0,1,2:T(8,128)(2,1)}, bf16[128,64,64]{0,1,2:T(8,128)(2,1)S(1)}, u32[]{:S(2)}) copy-start(bf16[128,64,64]{0,1,2:T(8,128)(2,1)S(1)} %fusion.12) | copy-start | bytes 3145732
  47.6 10.7 %copy-start.4 = (bf16[128,64,64]{0,1,2:T(8,128)(2,1)S(1)}, bf16[128,64,64]{0,1,2:T(8,128)(2,1)}, u32[]{:S(2)}) copy-start(bf16[128,64,64]{0,1,2:T(8,128)(2,1)} %copy-done.3) | copy-start | bytes 3145732
  122.5 11.3 %all-to-all-start.2 = ((f32[16,1,1024]{2,1,0:T(1,128)}), f32[16,1,1024]{2,1,0:T(1,128)S(1)}, u32[]{:S(2)}, u32[]{:S(2)}) async-start(f32[16,1,1024]{2,1,0:T(1,128)} %broadcast_in_dim.32), calls=%async_computation.2 | async-start | bytes 131072 | tf_op jit(solution)/shard_map/all_to_all | solution.py:117
  163.2 16.2 %copy-start.1 = (bf16[64,64,64]{2,1,0:T(8,128)(2,1)S(1)}, bf16[64,64,64]{2,1,0:T(8,128)(2,1)}, u32[]{:S(2)}) copy-start(bf16[64,64,64]{2,1,0:T(8,128)(2,1)} %param.13) | copy-start | bytes 1572868
Sparse Core Ops, SparseCore 0:
  11.0 61.7 all-gather.5
  74.6 88.5 all-gather.3
